TPU v7x, 128 devices: a whole 4x4x4 slice. The times are simulated.
128 devices in a mesh: sec: 2 (over z_hi), row: 8 (over z_lo, y), col: 8 (over x, core).
Axes of the slice: x: 4, y: 4, z: 4 (z_hi: 2, z_lo: 2; z = z_hi * 2 + z_lo), core: 2. Of those that a mesh axis runs over, the one named last changes fastest.
Arguments:
- left_feat: bfloat16 [320, 16, 2048], P(None, 'row', 'col'), may hold values from -8 to 8
- right_feat: bfloat16 [320, 16, 2048], P(None, 'row', 'col'), may hold values from -8 to 8
- offsets: int32 [8, 8], P('row', 'col'), may hold values from 0 to 79, as said below
- w_first: bfloat16 [32, 40, 3, 3, 3], replicated, may hold values from -0.1875 to 0.1875
- b_first: float32 [32], replicated, may hold values from -3 to 3
- w_second: bfloat16 [32, 32, 3, 3, 3], replicated, may hold values from -0.21875 to 0.21875
- b_second: float32 [32], replicated, may hold values from -3 to 3
- w_third: bfloat16 [32, 32, 3, 3, 3], replicated, may hold values from -0.21875 to 0.21875
- b_third: float32 [32], replicated, may hold values from -3 to 3
- w_out: bfloat16 [1, 32, 3, 3, 3], replicated, may hold values from -0.21875 to 0.21875
- b_out: float32 [1], replicated, may hold values from -3 to 3
Outputs:
- cost: float32 [48, 16, 2048], P('sec', 'row', 'col')
Inputs may be any that keep to these rules, and one draw needn't show every extreme that they name: `offsets`: one offset a tile; some tile has offset 0 and some tile has offset 80 - 1.
All inputs are finite; a program needn't handle non-finite values.
Results may differ from a plain program's by a relative error of at most 0.006.
Values may be sent and summed in bfloat16 or wider, within the bound.
No kernel may reach another device: no remote copies, remote signals or barrier semaphores. Data moves between devices by JAX's collectives and lax.ppermute only.
A program may use at most 128 MiB of HBM per device.

v0:
```python
import functools

import jax
import jax.numpy as jnp
from jax import lax
from jax.experimental import pallas as pl
from jax.sharding import PartitionSpec as P

G = 40
DISP = 48
GS = 8
EXT = 4
PRE = 136
LINE = 384
DEPTH = 32
STEP = 1536


def from_behind(array, axis, by):
    size = lax.axis_size(axis)
    pairs = [(i, i + by) for i in range(size) if 0 <= i + by < size]
    return lax.ppermute(array, axis, pairs)


def row_halo(cells):
    above = from_behind(cells[:, :, -1:], "row", 1)
    below = from_behind(cells[:, :, :1], "row", -1)
    return jnp.concatenate([above, cells, below], axis=2)


def inside(levels, width, ext):
    first_level = lax.axis_index("sec") * (DISP // lax.axis_size("sec"))
    first_col = lax.axis_index("col") * (width - 2 * ext)
    total = (width - 2 * ext) * lax.axis_size("col")
    level = first_level - ext + jnp.arange(levels)
    col = first_col - ext + jnp.arange(width)
    keep_level = (level >= 0) & (level < DISP)
    keep_col = (col >= 0) & (col < total)
    return keep_level[:, None, None] & keep_col[None, None, :]


def conv3(volume, kernel):
    out = lax.conv_general_dilated(
        volume[None],
        kernel,
        (1, 1, 1),
        "VALID",
        dimension_numbers=("NCDHW", "OIDHW", "NCDHW"),
        preferred_element_type=jnp.float32,
    )
    return out[0]


def correlate_kernel(left_ref, window_ref, out_ref):
    rows, _, _, width = left_ref.shape
    count = out_ref.shape[1]
    for row in range(rows):
        left = left_ref[row].astype(jnp.float32)
        window = window_ref[row].astype(jnp.float32)
        for level in range(count):
            begin = count - 1 - level
            product = left * window[:, :, begin : begin + width]
            summed = product.sum(axis=0)
            out_ref[row, level] = (summed / GS).astype(jnp.bfloat16)


def correlate(left, window, count, width):
    chans, rows, _ = left.shape

    def grouped(x):
        return jnp.transpose(x.reshape(G, GS, rows, x.shape[2]), (2, 1, 0, 3))

    out = pl.pallas_call(
        correlate_kernel,
        out_shape=jax.ShapeDtypeStruct((rows, count, G, width), jnp.bfloat16),
    )(grouped(left), grouped(window))
    return jnp.transpose(out, (2, 1, 0, 3))


def lanes(ref, start, size):
    limit = ref.shape[1]
    if start + size <= limit:
        return ref[:, start : start + size]
    rest = jnp.zeros((ref.shape[0], start + size - limit), ref.dtype)
    return jnp.concatenate([ref[:, start:limit], rest], axis=1)


def own_kernel(x_ref, w_ref, o_ref, *, cout):
    plane = DEPTH * LINE
    for row in range(w_ref.shape[0]):
        weights = w_ref[row]
        for base in range(0, plane, STEP):
            stacked = jnp.concatenate(
                [
                    lanes(x_ref, q * plane + a * LINE + base, STEP + 128)
                    for a in range(3)
                    for q in range(2)
                ],
                axis=0,
            )
            z = jnp.dot(weights, stacked, preferred_element_type=jnp.float32)
            out = z[0:cout, 0:STEP] + z[cout : 2 * cout, 1 : STEP + 1]
            out = out + z[2 * cout : 3 * cout, 2 : STEP + 2]
            o_ref[:, row * plane + base : row * plane + base + STEP] = out


def halo_kernel(above_ref, below_ref, w_ref, part_ref, b_ref, keep_ref, *rest, cout, relu, index):
    if len(rest) == 2:
        extra_ref, o_ref = rest
    else:
        extra_ref = None
        (o_ref,) = rest
    plane = DEPTH * LINE
    for row, halo_ref in ((0, above_ref), (1, below_ref)):
        weights = w_ref[row]
        for base in range(0, plane, STEP):
            stacked = jnp.concatenate(
                [lanes(halo_ref, a * LINE + base, STEP + 128) for a in range(3)],
                axis=0,
            )
            z = jnp.dot(weights, stacked, preferred_element_type=jnp.float32)
            out = z[0:cout, 0:STEP] + z[cout : 2 * cout, 1 : STEP + 1]
            out = out + z[2 * cout : 3 * cout, 2 : STEP + 2]
            at = row * plane + base
            out = out + part_ref[:, at : at + STEP] + b_ref[index, :cout]
            if extra_ref is not None:
                shifted = lanes(extra_ref, at + 2 * LINE, STEP + 128)[:, 2 : STEP + 2]
                out = out + shifted.astype(jnp.float32)
            if relu:
                out = jnp.maximum(out, 0.0)
            out = jnp.where(keep_ref[index : index + 1, at : at + STEP] > 0, out, 0.0)
            o_ref[:, at : at + STEP] = out.astype(o_ref.dtype)


def keep_lines(levels, cols, ext):
    first_level = lax.axis_index("sec") * (DISP // lax.axis_size("sec"))
    width = cols - 2 * ext
    first_col = lax.axis_index("col") * width
    total = width * lax.axis_size("col")
    level = first_level - ext + jnp.arange(DEPTH)
    col = first_col - ext + jnp.arange(LINE)
    keep_level = (level >= 0) & (level < DISP) & (jnp.arange(DEPTH) < levels)
    keep_col = (col >= 0) & (col < total) & (jnp.arange(LINE) < cols)
    return keep_level[:, None] & keep_col[None, :]


def conv_layer(own, levels, cols, sent, kernel, biases, keeps, index, extra=None, relu=True, out_dtype=jnp.bfloat16):
    chans = own.shape[0]
    plane = DEPTH * LINE
    cout, cin = kernel.shape[:2]
    rows_out = max(cout, 8)
    taps = jnp.transpose(kernel, (3, 4, 0, 2, 1))
    taps = jnp.pad(taps, ((0, 0), (0, 0), (0, rows_out - cout), (0, 0), (0, chans - cin)))
    own_taps = jnp.stack(
        [jnp.stack([taps[q + 1 - h] for q in range(2)], axis=3) for h in range(2)]
    ).reshape(2, 3 * rows_out, 6 * chans)
    halo_taps = jnp.stack([taps[0], taps[2]]).reshape(2, 3 * rows_out, 3 * chans)
    part = pl.pallas_call(
        functools.partial(own_kernel, cout=rows_out),
        out_shape=jax.ShapeDtypeStruct((rows_out, 2 * plane), jnp.float32),
    )(own, own_taps)
    span = levels * LINE
    pad = ((0, chans - sent), (0, plane - span))
    above = jnp.pad(from_behind(own[:sent, plane : plane + span], "row", 1), pad)
    below = jnp.pad(from_behind(own[:sent, :span], "row", -1), pad)
    operands = [above, below, halo_taps, part, biases, keeps]
    if extra is not None:
        operands.append(extra)
    out = pl.pallas_call(
        functools.partial(halo_kernel, cout=rows_out, relu=relu, index=index),
        out_shape=jax.ShapeDtypeStruct((rows_out, 2 * plane), out_dtype),
    )(*operands)
    return out[:cout]


def shards(
    left_feat,
    right_feat,
    offsets,
    w_first,
    b_first,
    w_second,
    b_second,
    w_third,
    b_third,
    w_out,
    b_out,
):
    chans, rows, width = left_feat.shape
    levels = DISP // lax.axis_size("sec")
    count = levels + 2 * EXT
    first_level = lax.axis_index("sec") * levels
    own_shift = offsets[0, 0]
    right_ext = jnp.concatenate(
        [
            from_behind(right_feat[:, :, width - PRE :], "col", 1),
            right_feat,
            jnp.zeros((chans, rows, 2 * EXT), right_feat.dtype),
        ],
        axis=2,
    )
    start = PRE - own_shift - first_level + EXT - (count - 1)
    window = lax.dynamic_slice_in_dim(right_ext, start, width + count - 1, axis=2)
    own_corr = correlate(left_feat, window, count, width)
    corr = jnp.concatenate(
        [
            from_behind(own_corr[..., width - EXT :], "col", 1),
            own_corr,
            from_behind(own_corr[..., :EXT], "col", -1),
        ],
        axis=3,
    )
    count_cols = width + 2 * EXT
    corr = jnp.transpose(corr, (0, 2, 1, 3))
    chans_in = -(-G // 16) * 16
    corr = jnp.pad(
        corr, ((0, chans_in - G), (0, 0), (0, DEPTH - count), (0, LINE - count_cols))
    )
    corr = jnp.where(keep_lines(count, count_cols, EXT), corr, 0.0).astype(jnp.bfloat16)

    sizes = [(count - 2 * k, count_cols - 2 * k) for k in range(EXT + 1)]
    flat = 2 * DEPTH * LINE

    def keep_of(k):
        return keep_lines(sizes[k][0], sizes[k][1], EXT - k)[None].repeat(2, 0).reshape(1, flat)

    keeps = jnp.concatenate(
        [keep_of(1), keep_of(2), keep_of(3), jnp.ones((1, flat), bool)], axis=0
    ).astype(jnp.float32)
    biases = [b_first, b_second, b_third, b_out]
    rows_b = max(b.shape[0] for b in biases)
    biases = jnp.stack([jnp.pad(b, (0, rows_b - b.shape[0])) for b in biases])[:, :, None]

    own = corr.reshape(corr.shape[0], flat)
    act_one = conv_layer(own, *sizes[0], G, w_first, biases, keeps, 0)
    act_two = conv_layer(act_one, *sizes[1], act_one.shape[0], w_second, biases, keeps, 1)
    act_three = conv_layer(
        act_two, *sizes[2], act_two.shape[0], w_third, biases, keeps, 2, extra=act_one
    )
    cost = cost_head(act_three, w_out, levels, width) + b_out[0]
    return jnp.transpose(cost, (1, 0, 2))


def cost_head(own, kernel, levels, width):
    chans = own.shape[0]
    plane = DEPTH * LINE
    cout, cin = kernel.shape[:2]
    rows_out = max(cout, 8)
    taps = jnp.transpose(kernel, (3, 4, 0, 2, 1))
    taps = jnp.pad(taps, ((0, 0), (0, 0), (0, rows_out - cout), (0, 0), (0, chans - cin)))
    nothing = jnp.zeros_like(taps[0])
    slots = [
        jnp.stack([taps[q + 1 - h] if 0 <= q + 1 - h <= 2 else nothing for q in range(2)], axis=3)
        for h in (-1, 0, 1, 2)
    ]
    head_taps = jnp.stack(slots).reshape(4, 3 * rows_out, 6 * chans)
    part = pl.pallas_call(
        functools.partial(own_kernel, cout=rows_out),
        out_shape=jax.ShapeDtypeStruct((rows_out, 4 * plane), jnp.float32),
    )(own, head_taps)
    part = part[0].reshape(4, DEPTH, LINE)[:, :levels, :width]
    from_above = from_behind(part[3], "row", 1)
    from_below = from_behind(part[0], "row", -1)
    return jnp.stack([part[1] + from_above, part[2] + from_below])


def solution(mesh):
    return jax.shard_map(
        shards,
        mesh=mesh,
        in_specs=(
            P(None, "row", "col"),
            P(None, "row", "col"),
            P("row", "col"),
            P(),
            P(),
            P(),
            P(),
            P(),
            P(),
            P(),
            P(),
        ),
        out_specs=P("sec", "row", "col"),
        check_vma=False,
    )
```

profile of v0, /device:TPU:100, one launch (start us, length us, event | category | flops | bytes accessed | tf_op | source)
XLA Modules:
  0.0 157.6 jit_solution(2719359267017967950)
XLA Ops:
  0.0 1.0 copy.71
  1.0 0.2 slice.121
  1.2 1.9 %collective-permute-start = (bf16[320,2,136]{2,0,1:T(8,128)(2,1)S(1)}, bf16[320,2,136]{2,0,1:T(8,128)(2,1)S(1)}, u32[]{:S(2)}, u32[]{:S(2)}) collective-permute-start(bf16[320,2,136]{2,0,1:T(8,128)(2,1)S(1)} %slice.121), channel_id=1, source_target_pairs={{0,1},{1,2},{2,3},{3,4},{4,5},{5,6},{6,7},{8,9},{9,10},{10,11},{11... | collective-permute-start | bytes 522248 | tf_op jit(solution)/shard_map/ppermute | solution.py:22
  3.8 1.8 %copy.121 = bf16[40,8,2,256]{3,0,1,2:T(8,128)(2,1)} copy(bf16[40,8,2,256]{3,2,1,0:T(2,128)(2,1)} %bitcast.102) | data formatting | bytes 655360 | tf_op jit(solution)/shard_map/reshape | solution.py:71
  6.0 3.6 %collective-permute-done = bf16[320,2,136]{2,0,1:T(8,128)(2,1)S(1)} collective-permute-done((bf16[320,2,136]{2,0,1:T(8,128)(2,1)S(1)}, bf16[320,2,136]{2,0,1:T(8,128)(2,1)S(1)}, u32[]{:S(2)}, u32[]{:S(2)}) %collective-permute-start) | collective-permute-done | bytes 174112 | tf_op jit(solution)/shard_map/ppermute | solution.py:22
  9.6 0.4 fusion.2
  10.0 0.9 copy.120
  10.8 6.2 %shard_map.109 = bf16[2,32,40,256]{3,2,1,0:T(8,128)(2,1)} custom-call(bf16[2,8,40,256]{3,2,1,0:T(8,128)(2,1)} %bitcast.101, bf16[2,8,40,287]{3,2,1,0:T(8,128)(2,1)} %bitcast.100), custom_call_target="tpu_custom_call" | custom-call | tf_op jit(solution)/shard_map/pallas_call | solution.py:73
  17.0 1.5 fusion.34
  18.6 0.5 copy.74
  19.1 1.9 %collective-permute-start.1 = (bf16[40,32,2,4]{0,1,3,2:T(8,128)(2,1)S(1)}, bf16[40,32,2,4]{0,1,3,2:T(8,128)(2,1)S(1)}, u32[]{:S(2)}, u32[]{:S(2)}) collective-permute-start(bf16[40,32,2,4]{0,1,3,2:T(8,128)(2,1)S(1)} %copy.74), channel_id=1, source_target_pairs={{0,1},{1,2},{2,3},{3,4},{4,5},{5,6},{6,7},{8,9},{9,10},{10,11},{11... | collective-permute-start | bytes 61448 | tf_op jit(solution)/shard_map/ppermute | solution.py:22
  21.1 0.5 copy.75
  21.6 3.6 %collective-permute-start.2 = (bf16[40,32,2,4]{0,1,3,2:T(8,128)(2,1)S(1)}, bf16[40,32,2,4]{0,1,3,2:T(8,128)(2,1)S(1)}, u32[]{:S(2)}, u32[]{:S(2)}) collective-permute-start(bf16[40,32,2,4]{0,1,3,2:T(8,128)(2,1)S(1)} %copy.75), channel_id=1, source_target_pairs={{1,0},{2,1},{3,2},{4,3},{5,4},{6,5},{7,6},{9,8},{10,9},{11,10},{12... | collective-permute-start | bytes 61448 | tf_op jit(solution)/shard_map/ppermute | solution.py:22
  25.6 0.5 copy.76
  26.1 1.0 collective-permute-done.2
  27.2 0.5 copy.77
  27.7 1.3 maximum_bitcast_fusion
  28.9 0.5 pad_select_fusion
  29.5 0.2 copy.116
  29.7 1.1 fusion.31
  30.8 0.6 copy-done
  31.5 3.6 %collective-permute-start.3 = (bf16[40,12288]{1,0:T(8,128)(2,1)}, bf16[40,12288]{1,0:T(8,128)(2,1)S(1)}, u32[]{:S(2)}, u32[]{:S(2)}) collective-permute-start(bf16[40,12288]{1,0:T(8,128)(2,1)} %get-tuple-element.6), channel_id=1, source_target_pairs={{0,8},{8,16},{16,24},{24,32},{32,40},{40,48},{48,56},{1,9},{9,17},... | collective-permute-start | bytes 2949128 | tf_op jit(solution)/shard_map/ppermute | solution.py:22
  35.1 4.6 %collective-permute-start.4 = (bf16[40,12288]{1,0:T(8,128)(2,1)S(1)}, bf16[40,12288]{1,0:T(8,128)(2,1)S(1)}, u32[]{:S(2)}, u32[]{:S(2)}) collective-permute-start(bf16[40,12288]{1,0:T(8,128)(2,1)S(1)} %get-tuple-element.5), channel_id=1, source_target_pairs={{8,0},{16,8},{24,16},{32,24},{40,32},{48,40},{56,48},{9,1},{17,9},... | collective-permute-start | bytes 2949128 | tf_op jit(solution)/shard_map/ppermute | solution.py:22
  39.7 1.2 add_convert_fusion.keep_ref
  41.7 0.8 reshape.152.w_ref
  43.2 0.7 copy.84.b_ref
  43.9 0.7 pad_maximum_fusion.3.w_ref
  44.6 7.3 %shard_map.110.part_ref = f32[32,24576]{1,0:T(8,128)} custom-call(bf16[48,24576]{1,0:T(8,128)(2,1)} %bitcast.96, bf16[2,96,288]{2,1,0:T(8,128)(2,1)} %pad_maximum_fusion.3.w_ref), custom_call_target="tpu_custom_call" | custom-call | tf_op jit(solution)/shard_map/pallas_call | solution.py:158
  51.9 8.1 %collective-permute-done.3 = bf16[40,12288]{1,0:T(8,128)(2,1)S(1)} collective-permute-done((bf16[40,12288]{1,0:T(8,128)(2,1)}, bf16[40,12288]{1,0:T(8,128)(2,1)S(1)}, u32[]{:S(2)}, u32[]{:S(2)}) %collective-permute-start.3) | collective-permute-done | bytes 983072 | tf_op jit(solution)/shard_map/ppermute | solution.py:22
  60.0 1.1 pad.40.above_ref
  61.2 0.4 collective-permute-done.4
  61.6 1.1 pad.41.below_ref
  62.7 6.2 %shard_map.111.x_ref.rest_0_ = bf16[32,24576]{1,0:T(8,128)(2,1)} custom-call(bf16[48,12288]{1,0:T(8,128)(2,1)} %pad.40.above_ref, bf16[48,12288]{1,0:T(8,128)(2,1)} %pad.41.below_ref, bf16[2,96,144]{2,1,0:T(8,128)(2,1)} %reshape.152.w_ref, f32[32,24576]{1,0:T(8,128)} %shard_map.110.part_ref, f32[4,32,1]{2,1,0:T(8,128)} %copy.84.b_ref, ...), custom_call_target="tpu_custom_call" | custom-call | tf_op jit(solution)/shard_map/pallas_call | solution.py:169
  68.9 1.5 fusion.33
  70.4 3.4 %collective-permute-start.5 = (bf16[32,11520]{1,0:T(8,128)(2,1)S(1)}, bf16[32,11520]{1,0:T(8,128)(2,1)S(1)}, u32[]{:S(2)}, u32[]{:S(2)}) collective-permute-start(bf16[32,11520]{1,0:T(8,128)(2,1)S(1)} %get-tuple-element.10), channel_id=1, source_target_pairs={{0,8},{8,16},{16,24},{24,32},{32,40},{40,48},{48,56},{1,9},{9,17},... | collective-permute-start | bytes 2211848 | tf_op jit(solution)/shard_map/ppermute | solution.py:22
  73.8 5.0 %collective-permute-start.6 = (bf16[32,11520]{1,0:T(8,128)(2,1)S(1)}, bf16[32,11520]{1,0:T(8,128)(2,1)S(1)}, u32[]{:S(2)}, u32[]{:S(2)}) collective-permute-start(bf16[32,11520]{1,0:T(8,128)(2,1)S(1)} %get-tuple-element.9), channel_id=1, source_target_pairs={{8,0},{16,8},{24,16},{32,24},{40,32},{48,40},{56,48},{9,1},{17,9},... | collective-permute-start | bytes 2211848 | tf_op jit(solution)/shard_map/ppermute | solution.py:22
  79.0 0.1 stack.118
  79.6 0.8 reshape.153.w_ref
  80.4 0.7 pad_maximum_fusion.10.w_ref
  81.0 1.0 slice_bitcast_fusion.2
  82.0 5.1 %shard_map.112.part_ref = f32[32,24576]{1,0:T(8,128)} custom-call(bf16[32,24576]{1,0:T(8,128)(2,1)} %shard_map.111.x_ref.rest_0_, bf16[2,96,192]{2,1,0:T(8,128)(2,1)} %pad_maximum_fusion.10.w_ref), custom_call_target="tpu_custom_call" | custom-call | tf_op jit(solution)/shard_map/pallas_call | solution.py:158
  87.2 6.4 %collective-permute-done.5 = bf16[32,11520]{1,0:T(8,128)(2,1)S(1)} collective-permute-done((bf16[32,11520]{1,0:T(8,128)(2,1)S(1)}, bf16[32,11520]{1,0:T(8,128)(2,1)S(1)}, u32[]{:S(2)}, u32[]{:S(2)}) %collective-permute-start.5) | collective-permute-done | bytes 737312 | tf_op jit(solution)/shard_map/ppermute | solution.py:22
  93.6 0.9 pad.44.above_ref
  94.6 0.2 collective-permute-done.6
  94.8 0.9 pad.45.below_ref
  95.7 5.9 %shard_map.113.x_ref = bf16[32,24576]{1,0:T(8,128)(2,1)} custom-call(bf16[32,12288]{1,0:T(8,128)(2,1)} %pad.44.above_ref, bf16[32,12288]{1,0:T(8,128)(2,1)} %pad.45.below_ref, bf16[2,96,96]{2,1,0:T(8,128)(2,1)} %reshape.153.w_ref, f32[32,24576]{1,0:T(8,128)} %shard_map.112.part_ref, f32[4,32,1]{2,1,0:T(8,128)} %copy.84.b_ref, ...), custom_call_target="tpu_custom_call" | custom-call | tf_op jit(solution)/shard_map/pallas_call | solution.py:169
  101.7 1.4 fusion.32
  103.1 2.3 %collective-permute-start.7 = (bf16[32,10752]{1,0:T(8,128)(2,1)S(1)}, bf16[32,10752]{1,0:T(8,128)(2,1)S(1)}, u32[]{:S(2)}, u32[]{:S(2)}) collective-permute-start(bf16[32,10752]{1,0:T(8,128)(2,1)S(1)} %get-tuple-element.8), channel_id=1, source_target_pairs={{0,8},{8,16},{16,24},{24,32},{32,40},{40,48},{48,56},{1,9},{9,17},... | collective-permute-start | bytes 2064392 | tf_op jit(solution)/shard_map/ppermute | solution.py:22
  105.4 6.4 %collective-permute-start.8 = (bf16[32,10752]{1,0:T(8,128)(2,1)S(1)}, bf16[32,10752]{1,0:T(8,128)(2,1)S(1)}, u32[]{:S(2)}, u32[]{:S(2)}) collective-permute-start(bf16[32,10752]{1,0:T(8,128)(2,1)S(1)} %get-tuple-element.7), channel_id=1, source_target_pairs={{8,0},{16,8},{24,16},{32,24},{40,32},{48,40},{56,48},{9,1},{17,9},... | collective-permute-start | bytes 2064392 | tf_op jit(solution)/shard_map/ppermute | solution.py:22
  112.5 0.8 reshape.154.w_ref
  114.0 0.6 pad_maximum_fusion.14.w_ref
  114.7 0.7 pad_maximum_fusion.11.w_ref
  115.3 5.1 %shard_map.114.part_ref = f32[32,24576]{1,0:T(8,128)} custom-call(bf16[32,24576]{1,0:T(8,128)(2,1)} %shard_map.113.x_ref, bf16[2,96,192]{2,1,0:T(8,128)(2,1)} %pad_maximum_fusion.11.w_ref), custom_call_target="tpu_custom_call" | custom-call | tf_op jit(solution)/shard_map/pallas_call | solution.py:158
  120.4 4.0 %collective-permute-done.7 = bf16[32,10752]{1,0:T(8,128)(2,1)S(1)} collective-permute-done((bf16[32,10752]{1,0:T(8,128)(2,1)S(1)}, bf16[32,10752]{1,0:T(8,128)(2,1)S(1)}, u32[]{:S(2)}, u32[]{:S(2)}) %collective-permute-start.7) | collective-permute-done | bytes 688160 | tf_op jit(solution)/shard_map/ppermute | solution.py:22
  124.4 0.9 pad.46.above_ref
  125.4 0.2 collective-permute-done.8
  125.6 0.9 pad.47.below_ref
  126.6 7.1 %shard_map.115.x_ref = bf16[32,24576]{1,0:T(8,128)(2,1)} custom-call(bf16[32,12288]{1,0:T(8,128)(2,1)} %pad.46.above_ref, bf16[32,12288]{1,0:T(8,128)(2,1)} %pad.47.below_ref, bf16[2,96,96]{2,1,0:T(8,128)(2,1)} %reshape.154.w_ref, f32[32,24576]{1,0:T(8,128)} %shard_map.114.part_ref, f32[4,32,1]{2,1,0:T(8,128)} %copy.84.b_ref, ...), custom_call_target="tpu_custom_call" | custom-call | tf_op jit(solution)/shard_map/pallas_call | solution.py:169
  133.7 6.8 %shard_map.116 = f32[8,49152]{1,0:T(8,128)} custom-call(bf16[32,24576]{1,0:T(8,128)(2,1)} %shard_map.115.x_ref, bf16[4,24,192]{2,1,0:T(8,128)(2,1)} %pad_maximum_fusion.14.w_ref), custom_call_target="tpu_custom_call" | custom-call | tf_op jit(solution)/shard_map/pallas_call | solution.py:257
  140.6 1.9 %slice_reduce_fusion = f32[49152]{0:T(1024)S(1)} fusion(f32[8,49152]{1,0:T(8,128)} %shard_map.116), kind=kLoop, calls=%fused_computation.10 | loop fusion | bytes 393216 | tf_op jit(solution)/shard_map/slice | solution.py:261
  142.5 6.5 %collective-permute-start.10 = (f32[24,256]{1,0:T(8,128)S(1)}, f32[24,256]{1,0:T(8,128)S(1)}, u32[]{:S(2)}, u32[]{:S(2)}) collective-permute-start(f32[24,256]{1,0:T(8,128)S(1)} %get-tuple-element.31), channel_id=1, source_target_pairs={{8,0},{16,8},{24,16},{32,24},{40,32},{48,40},{56,48},{9,1},{17,9},... | collective-permute-start | bytes 73736 | tf_op jit(solution)/shard_map/ppermute | solution.py:22
  149.0 1.9 %collective-permute-start.9 = (f32[24,256]{1,0:T(8,128)S(1)}, f32[24,256]{1,0:T(8,128)S(1)}, u32[]{:S(2)}, u32[]{:S(2)}) collective-permute-start(f32[24,256]{1,0:T(8,128)S(1)} %get-tuple-element.30), channel_id=1, source_target_pairs={{0,8},{8,16},{16,24},{24,32},{32,40},{40,48},{48,56},{1,9},{9,17},... | collective-permute-start | bytes 73736 | tf_op jit(solution)/shard_map/ppermute | solution.py:22
  151.0 5.9 %collective-permute-done.9 = f32[24,256]{1,0:T(8,128)S(1)} collective-permute-done((f32[24,256]{1,0:T(8,128)S(1)}, f32[24,256]{1,0:T(8,128)S(1)}, u32[]{:S(2)}, u32[]{:S(2)}) %collective-permute-start.9) | collective-permute-done | bytes 24608 | tf_op jit(solution)/shard_map/ppermute | solution.py:22
  156.9 0.7 fusion.4
  (78 shorter events, 3.7 us)
Async XLA Ops:
  1.2 8.4 %collective-permute-start = (bf16[320,2,136]{2,0,1:T(8,128)(2,1)S(1)}, bf16[320,2,136]{2,0,1:T(8,128)(2,1)S(1)}, u32[]{:S(2)}, u32[]{:S(2)}) collective-permute-start(bf16[320,2,136]{2,0,1:T(8,128)(2,1)S(1)} %slice.121), channel_id=1, source_target_pairs={{0,1},{1,2},{2,3},{3,4},{4,5},{5,6},{6,7},{8,9},{9,10},{10,11},{11... | collective-permute-start | bytes 522248 | tf_op jit(solution)/shard_map/ppermute | solution.py:22
  18.6 9.1 %copy-start.1 = (bf16[2,32,40,256]{3,2,1,0:T(8,128)(2,1)S(1)}, bf16[2,32,40,256]{3,2,1,0:T(8,128)(2,1)}, u32[]{:S(2)}) copy-start(bf16[2,32,40,256]{3,2,1,0:T(8,128)(2,1)} %shard_map.109) | copy-start | bytes 3932164
  19.1 6.5 %collective-permute-start.1 = (bf16[40,32,2,4]{0,1,3,2:T(8,128)(2,1)S(1)}, bf16[40,32,2,4]{0,1,3,2:T(8,128)(2,1)S(1)}, u32[]{:S(2)}, u32[]{:S(2)}) collective-permute-start(bf16[40,32,2,4]{0,1,3,2:T(8,128)(2,1)S(1)} %copy.74), channel_id=1, source_target_pairs={{0,1},{1,2},{2,3},{3,4},{4,5},{5,6},{6,7},{8,9},{9,10},{10,11},{11... | collective-permute-start | bytes 61448 | tf_op jit(solution)/shard_map/ppermute | solution.py:22
  21.6 5.5 %collective-permute-start.2 = (bf16[40,32,2,4]{0,1,3,2:T(8,128)(2,1)S(1)}, bf16[40,32,2,4]{0,1,3,2:T(8,128)(2,1)S(1)}, u32[]{:S(2)}, u32[]{:S(2)}) collective-permute-start(bf16[40,32,2,4]{0,1,3,2:T(8,128)(2,1)S(1)} %copy.75), channel_id=1, source_target_pairs={{1,0},{2,1},{3,2},{4,3},{5,4},{6,5},{7,6},{9,8},{10,9},{11,10},{12... | collective-permute-start | bytes 61448 | tf_op jit(solution)/shard_map/ppermute | solution.py:22
  29.7 1.7 %copy-start = (bf16[6,8,64,384]{3,1,2,0:T(8,128)(2,1)}, bf16[6,8,64,384]{3,1,2,0:T(8,128)(2,1)S(1)}, u32[]{:S(2)}) copy-start(bf16[6,8,64,384]{3,1,2,0:T(8,128)(2,1)S(1)} %copy.116) | copy-start | bytes 7077892
  29.7 11.2 %copy-start.2 = (bf16[32,40,3,3,3]{1,0,4,3,2:T(8,128)(2,1)S(1)}, bf16[32,40,3,3,3]{1,0,4,3,2:T(8,128)(2,1)}, u32[]{:S(2)}) copy-start(bf16[32,40,3,3,3]{1,0,4,3,2:T(8,128)(2,1)} %param.14) | copy-start | bytes 207364
  31.5 11.7 %copy-start.5 = (f32[32]{0:T(128)S(1)}, f32[32]{0:T(128)}, u32[]{:S(2)}) copy-start(f32[32]{0:T(128)} %param.19) | copy-start | bytes 388
  31.5 11.7 %copy-start.6 = (f32[32]{0:T(128)S(1)}, f32[32]{0:T(128)}, u32[]{:S(2)}) copy-start(f32[32]{0:T(128)} %param.17) | copy-start | bytes 388
  31.5 11.7 %copy-start.7 = (f32[32]{0:T(128)S(1)}, f32[32]{0:T(128)}, u32[]{:S(2)}) copy-start(f32[32]{0:T(128)} %param.15) | copy-start | bytes 388
  31.5 28.6 %collective-permute-start.3 = (bf16[40,12288]{1,0:T(8,128)(2,1)}, bf16[40,12288]{1,0:T(8,128)(2,1)S(1)}, u32[]{:S(2)}, u32[]{:S(2)}) collective-permute-start(bf16[40,12288]{1,0:T(8,128)(2,1)} %get-tuple-element.6), channel_id=1, source_target_pairs={{0,8},{8,16},{16,24},{24,32},{32,40},{40,48},{48,56},{1,9},{9,17},... | collective-permute-start | bytes 2949128 | tf_op jit(solution)/shard_map/ppermute | solution.py:22
  35.1 26.5 %collective-permute-start.4 = (bf16[40,12288]{1,0:T(8,128)(2,1)S(1)}, bf16[40,12288]{1,0:T(8,128)(2,1)S(1)}, u32[]{:S(2)}, u32[]{:S(2)}) collective-permute-start(bf16[40,12288]{1,0:T(8,128)(2,1)S(1)} %get-tuple-element.5), channel_id=1, source_target_pairs={{8,0},{16,8},{24,16},{32,24},{40,32},{48,40},{56,48},{9,1},{17,9},... | collective-permute-start | bytes 2949128 | tf_op jit(solution)/shard_map/ppermute | solution.py:22
  68.9 9.9 %copy-start.3 = (bf16[32,32,3,3,3]{1,0,4,3,2:T(8,128)(2,1)S(1)}, bf16[32,32,3,3,3]{1,0,4,3,2:T(8,128)(2,1)}, u32[]{:S(2)}) copy-start(bf16[32,32,3,3,3]{1,0,4,3,2:T(8,128)(2,1)} %param.16) | copy-start | bytes 165892
  70.4 23.3 %collective-permute-start.5 = (bf16[32,11520]{1,0:T(8,128)(2,1)S(1)}, bf16[32,11520]{1,0:T(8,128)(2,1)S(1)}, u32[]{:S(2)}, u32[]{:S(2)}) collective-permute-start(bf16[32,11520]{1,0:T(8,128)(2,1)S(1)} %get-tuple-element.10), channel_id=1, source_target_pairs={{0,8},{8,16},{16,24},{24,32},{32,40},{40,48},{48,56},{1,9},{9,17},... | collective-permute-start | bytes 2211848 | tf_op jit(solution)/shard_map/ppermute | solution.py:22
  73.8 21.0 %collective-permute-start.6 = (bf16[32,11520]{1,0:T(8,128)(2,1)S(1)}, bf16[32,11520]{1,0:T(8,128)(2,1)S(1)}, u32[]{:S(2)}, u32[]{:S(2)}) collective-permute-start(bf16[32,11520]{1,0:T(8,128)(2,1)S(1)} %get-tuple-element.9), channel_id=1, source_target_pairs={{8,0},{16,8},{24,16},{32,24},{40,32},{48,40},{56,48},{9,1},{17,9},... | collective-permute-start | bytes 2211848 | tf_op jit(solution)/shard_map/ppermute | solution.py:22
  101.7 11.6 %copy-start.4 = (bf16[1,32,3,3,3]{1,4,3,2,0:T(4,128)(2,1)S(1)}, bf16[1,32,3,3,3]{1,4,3,2,0:T(4,128)(2,1)}, u32[]{:S(2)}) copy-start(bf16[1,32,3,3,3]{1,4,3,2,0:T(4,128)(2,1)} %param.20) | copy-start | bytes 5188
  103.1 21.4 %collective-permute-start.7 = (bf16[32,10752]{1,0:T(8,128)(2,1)S(1)}, bf16[32,10752]{1,0:T(8,128)(2,1)S(1)}, u32[]{:S(2)}, u32[]{:S(2)}) collective-permute-start(bf16[32,10752]{1,0:T(8,128)(2,1)S(1)} %get-tuple-element.8), channel_id=1, source_target_pairs={{0,8},{8,16},{16,24},{24,32},{32,40},{40,48},{48,56},{1,9},{9,17},... | collective-permute-start | bytes 2064392 | tf_op jit(solution)/shard_map/ppermute | solution.py:22
  105.4 20.2 %collective-permute-start.8 = (bf16[32,10752]{1,0:T(8,128)(2,1)S(1)}, bf16[32,10752]{1,0:T(8,128)(2,1)S(1)}, u32[]{:S(2)}, u32[]{:S(2)}) collective-permute-start(bf16[32,10752]{1,0:T(8,128)(2,1)S(1)} %get-tuple-element.7), channel_id=1, source_target_pairs={{8,0},{16,8},{24,16},{32,24},{40,32},{48,40},{56,48},{9,1},{17,9},... | collective-permute-start | bytes 2064392 | tf_op jit(solution)/shard_map/ppermute | solution.py:22
  142.5 8.4 %collective-permute-start.10 = (f32[24,256]{1,0:T(8,128)S(1)}, f32[24,256]{1,0:T(8,128)S(1)}, u32[]{:S(2)}, u32[]{:S(2)}) collective-permute-start(f32[24,256]{1,0:T(8,128)S(1)} %get-tuple-element.31), channel_id=1, source_target_pairs={{8,0},{16,8},{24,16},{32,24},{40,32},{48,40},{56,48},{9,1},{17,9},... | collective-permute-start | bytes 73736 | tf_op jit(solution)/shard_map/ppermute | solution.py:22
  149.0 7.8 %collective-permute-start.9 = (f32[24,256]{1,0:T(8,128)S(1)}, f32[24,256]{1,0:T(8,128)S(1)}, u32[]{:S(2)}, u32[]{:S(2)}) collective-permute-start(f32[24,256]{1,0:T(8,128)S(1)} %get-tuple-element.30), channel_id=1, source_target_pairs={{0,8},{8,16},{16,24},{24,32},{32,40},{40,48},{48,56},{1,9},{9,17},... | collective-permute-start | bytes 73736 | tf_op jit(solution)/shard_map/ppermute | solution.py:22
where the time goes:
time: 158 us
  Pallas kernels  49.9 us (32%)
  starting transfers between devices  41.2 us (26%)
  waiting for transfers between devices  29.9 us (19%)
  local copies, waits for them, and re-layouts  27.3 us (17%)
  other arithmetic  7.38 us (5%)
  between operations  1.88 us (1%)
    ppermute x11, starting transfers between devices, from_behind(): return lax.ppermute(array, axis, pairs)  41.2 us
    ppermute x11, waiting for transfers between devices, from_behind(): return lax.ppermute(array, axis, pairs)  29.9 us
    pallas_call x3, Pallas kernels, conv_layer(): pl.pallas_call(functools.partial(halo_kernel, cout=rows_out, relu=relu, i...  19.3 us
    pallas_call x3, Pallas kernels, conv_layer(): pl.pallas_call(functools.partial(own_kernel, cout=rows_out), out_shape=ja...  17.6 us
    pallas_call x1, Pallas kernels, cost_head(): pl.pallas_call(functools.partial(own_kernel, cout=rows_out), out_shape=ja...  6.84 us
    pallas_call x1, Pallas kernels, correlate(): pl.pallas_call(correlate_kernel, out_shape=jax.ShapeDtypeStruct((rows, co...  6.21 us
    slice x3, local copies, waits for them, and re-layouts, conv_layer(): below = jnp.pad(from_behind(own[:sent, :span], 'row', -1), pad)  3.99 us
  transfers between devices with their start and end apart: 11, of which 9 were waited for; matrix products, arithmetic and copies ran while one was open for 11% of the time, Pallas kernels for 11%

commit v1 on v0

--- a/solution.py
+++ b/solution.py
@@ -85,16 +85,16 @@
     return jnp.concatenate([ref[:, start:limit], rest], axis=1)
 
 
-def own_kernel(x_ref, w_ref, o_ref, *, cout):
+def own_kernel(x0_ref, x1_ref, w_ref, o_ref, *, cout):
     plane = DEPTH * LINE
     for row in range(w_ref.shape[0]):
         weights = w_ref[row]
         for base in range(0, plane, STEP):
             stacked = jnp.concatenate(
                 [
-                    lanes(x_ref, q * plane + a * LINE + base, STEP + 128)
+                    lanes(x_ref, a * LINE + base, STEP + 128)
                     for a in range(3)
-                    for q in range(2)
+                    for x_ref in (x0_ref, x1_ref)
                 ],
                 axis=0,
             )
@@ -104,32 +104,30 @@
             o_ref[:, row * plane + base : row * plane + base + STEP] = out
 
 
-def halo_kernel(above_ref, below_ref, w_ref, part_ref, b_ref, keep_ref, *rest, cout, relu, index):
+def halo_kernel(halo_ref, w_ref, part_ref, b_ref, keep_ref, *rest, cout, relu, index, row):
     if len(rest) == 2:
         extra_ref, o_ref = rest
     else:
         extra_ref = None
         (o_ref,) = rest
     plane = DEPTH * LINE
-    for row, halo_ref in ((0, above_ref), (1, below_ref)):
-        weights = w_ref[row]
-        for base in range(0, plane, STEP):
-            stacked = jnp.concatenate(
-                [lanes(halo_ref, a * LINE + base, STEP + 128) for a in range(3)],
-                axis=0,
-            )
-            z = jnp.dot(weights, stacked, preferred_element_type=jnp.float32)
-            out = z[0:cout, 0:STEP] + z[cout : 2 * cout, 1 : STEP + 1]
-            out = out + z[2 * cout : 3 * cout, 2 : STEP + 2]
-            at = row * plane + base
-            out = out + part_ref[:, at : at + STEP] + b_ref[index, :cout]
-            if extra_ref is not None:
-                shifted = lanes(extra_ref, at + 2 * LINE, STEP + 128)[:, 2 : STEP + 2]
-                out = out + shifted.astype(jnp.float32)
-            if relu:
-                out = jnp.maximum(out, 0.0)
-            out = jnp.where(keep_ref[index : index + 1, at : at + STEP] > 0, out, 0.0)
-            o_ref[:, at : at + STEP] = out.astype(o_ref.dtype)
+    weights = w_ref[row]
+    for base in range(0, plane, STEP):
+        stacked = jnp.concatenate(
+            [lanes(halo_ref, a * LINE + base, STEP + 128) for a in range(3)], axis=0
+        )
+        z = jnp.dot(weights, stacked, preferred_element_type=jnp.float32)
+        out = z[0:cout, 0:STEP] + z[cout : 2 * cout, 1 : STEP + 1]
+        out = out + z[2 * cout : 3 * cout, 2 : STEP + 2]
+        at = row * plane + base
+        out = out + part_ref[:, at : at + STEP] + b_ref[index, :cout]
+        if extra_ref is not None:
+            shifted = lanes(extra_ref, base + 2 * LINE, STEP + 128)[:, 2 : STEP + 2]
+            out = out + shifted.astype(jnp.float32)
+        if relu:
+            out = jnp.maximum(out, 0.0)
+        out = jnp.where(keep_ref[index : index + 1, at : at + STEP] > 0, out, 0.0)
+        o_ref[:, base : base + STEP] = out.astype(o_ref.dtype)
 
 
 def keep_lines(levels, cols, ext):
@@ -145,7 +143,7 @@
 
 
 def conv_layer(own, levels, cols, sent, kernel, biases, keeps, index, extra=None, relu=True, out_dtype=jnp.bfloat16):
-    chans = own.shape[0]
+    chans = own[0].shape[0]
     plane = DEPTH * LINE
     cout, cin = kernel.shape[:2]
     rows_out = max(cout, 8)
@@ -158,19 +156,22 @@
     part = pl.pallas_call(
         functools.partial(own_kernel, cout=rows_out),
         out_shape=jax.ShapeDtypeStruct((rows_out, 2 * plane), jnp.float32),
-    )(own, own_taps)
+    )(*own, own_taps)
     span = levels * LINE
     pad = ((0, chans - sent), (0, plane - span))
-    above = jnp.pad(from_behind(own[:sent, plane : plane + span], "row", 1), pad)
-    below = jnp.pad(from_behind(own[:sent, :span], "row", -1), pad)
-    operands = [above, below, halo_taps, part, biases, keeps]
-    if extra is not None:
-        operands.append(extra)
-    out = pl.pallas_call(
-        functools.partial(halo_kernel, cout=rows_out, relu=relu, index=index),
-        out_shape=jax.ShapeDtypeStruct((rows_out, 2 * plane), out_dtype),
-    )(*operands)
-    return out[:cout]
+    above = jnp.pad(from_behind(own[1][:sent, :span], "row", 1), pad)
+    below = jnp.pad(from_behind(own[0][:sent, :span], "row", -1), pad)
+    planes = []
+    for row, halo in ((0, above), (1, below)):
+        operands = [halo, halo_taps, part, biases, keeps]
+        if extra is not None:
+            operands.append(extra[row])
+        out = pl.pallas_call(
+            functools.partial(halo_kernel, cout=rows_out, relu=relu, index=index, row=row),
+            out_shape=jax.ShapeDtypeStruct((rows_out, plane), out_dtype),
+        )(*operands)
+        planes.append(out[:cout])
+    return planes
 
 
 def shards(
@@ -231,18 +232,18 @@
     rows_b = max(b.shape[0] for b in biases)
     biases = jnp.stack([jnp.pad(b, (0, rows_b - b.shape[0])) for b in biases])[:, :, None]
 
-    own = corr.reshape(corr.shape[0], flat)
+    own = [corr[:, 0].reshape(corr.shape[0], flat // 2), corr[:, 1].reshape(corr.shape[0], flat // 2)]
     act_one = conv_layer(own, *sizes[0], G, w_first, biases, keeps, 0)
-    act_two = conv_layer(act_one, *sizes[1], act_one.shape[0], w_second, biases, keeps, 1)
+    act_two = conv_layer(act_one, *sizes[1], act_one[0].shape[0], w_second, biases, keeps, 1)
     act_three = conv_layer(
-        act_two, *sizes[2], act_two.shape[0], w_third, biases, keeps, 2, extra=act_one
+        act_two, *sizes[2], act_two[0].shape[0], w_third, biases, keeps, 2, extra=act_one
     )
     cost = cost_head(act_three, w_out, levels, width) + b_out[0]
     return jnp.transpose(cost, (1, 0, 2))
 
 
 def cost_head(own, kernel, levels, width):
-    chans = own.shape[0]
+    chans = own[0].shape[0]
     plane = DEPTH * LINE
     cout, cin = kernel.shape[:2]
     rows_out = max(cout, 8)
@@ -257,7 +258,7 @@
     part = pl.pallas_call(
         functools.partial(own_kernel, cout=rows_out),
         out_shape=jax.ShapeDtypeStruct((rows_out, 4 * plane), jnp.float32),
-    )(own, head_taps)
+    )(*own, head_taps)
     part = part[0].reshape(4, DEPTH, LINE)[:, :levels, :width]
     from_above = from_behind(part[3], "row", 1)
     from_below = from_behind(part[0], "row", -1)

time: 158 us -> 160 us (1.013)
  waiting for transfers between devices: 29.9 us -> 20.1 us
  Pallas kernels: 49.9 us -> 57.9 us
  starting transfers between devices: 41.2 us -> 35.5 us
  local copies, waits for them, and re-layouts: 27.3 us -> 32.8 us
  other arithmetic: 7.38 us -> 9.87 us
    ppermute x11, waiting for transfers between devices: 29.9 us -> 20.1 us  [from_behind(): return lax.ppermute(array, axis, pairs)]
    pallas_call x3 -> x6, Pallas kernels: 19.3 us -> 27.6 us  [conv_layer(): pl.pallas_call(functools.partial(halo_kernel, cout=rows_out, relu=relu, i...]
    ppermute x11, starting transfers between devices: 41.2 us -> 35.5 us  [from_behind(): return lax.ppermute(array, axis, pairs)]
    unnamed x20 -> x27, local copies, waits for them, and re-layouts: 1.96 us -> 5.71 us
    slice x3 -> x6, local copies, waits for them, and re-layouts: 3.99 us -> 1.73 us  [the longest x2 1.2 us: conv_layer(): above = jnp.pad(from_behind(own[1][:sent, :span], 'row', 1), pad)]
  transfers between devices with their start and end apart: 11 -> 11, of which waited for: 9 -> 7; matrix products, arithmetic and copies ran while one was open for 11% -> 18% of each run, Pallas kernels for 11% -> 20%
where the time goes in v1:
time: 160 us; the launch traced here: 158 us
  Pallas kernels  57.9 us (36%)
  starting transfers between devices  35.5 us (22%)
  local copies, waits for them, and re-layouts  32.8 us (20%)
  waiting for transfers between devices  20.1 us (13%)
  other arithmetic  9.87 us (6%)
  between operations  1.87 us (1%)
    ppermute x11, starting transfers between devices, from_behind(): return lax.ppermute(array, axis, pairs)  35.5 us
    pallas_call x6, Pallas kernels, conv_layer(): pl.pallas_call(functools.partial(halo_kernel, cout=rows_out, relu=relu, i...  27.6 us
    ppermute x11, waiting for transfers between devices, from_behind(): return lax.ppermute(array, axis, pairs)  20.1 us
    pallas_call x3, Pallas kernels, conv_layer(): pl.pallas_call(functools.partial(own_kernel, cout=rows_out), out_shape=ja...  17.4 us
    pallas_call x1, Pallas kernels, cost_head(): pl.pallas_call(functools.partial(own_kernel, cout=rows_out), out_shape=ja...  6.71 us
    pallas_call x1, Pallas kernels, correlate(): pl.pallas_call(correlate_kernel, out_shape=jax.ShapeDtypeStruct((rows, co...  6.21 us
    unnamed x27, local copies, waits for them, and re-layouts  5.71 us
    pad x3, local copies, waits for them, and re-layouts, conv_layer(): below = jnp.pad(from_behind(own[0][:sent, :span], 'row', -1), pad)  4.26 us
  transfers between devices with their start and end apart: 11, of which 7 were waited for; matrix products, arithmetic and copies ran while one was open for 18% of the time, Pallas kernels for 20%

profile of v1, /device:TPU:100, one launch (start us, length us, event | category | flops | bytes accessed | tf_op | source)
XLA Modules:
  0.0 158.0 jit_solution(7530220053452879633)
XLA Ops:
  0.0 1.0 copy.83
  1.2 1.9 %collective-permute-start = (bf16[320,2,136]{2,0,1:T(8,128)(2,1)S(1)}, bf16[320,2,136]{2,0,1:T(8,128)(2,1)S(1)}, u32[]{:S(2)}, u32[]{:S(2)}) collective-permute-start(bf16[320,2,136]{2,0,1:T(8,128)(2,1)S(1)} %slice.139), channel_id=1, source_target_pairs={{0,1},{1,2},{2,3},{3,4},{4,5},{5,6},{6,7},{8,9},{9,10},{10,11},{11... | collective-permute-start | bytes 522248 | tf_op jit(solution)/shard_map/ppermute | solution.py:22
  3.8 1.8 %copy.145 = bf16[40,8,2,256]{3,0,1,2:T(8,128)(2,1)} copy(bf16[40,8,2,256]{3,2,1,0:T(2,128)(2,1)} %bitcast.121) | data formatting | bytes 655360 | tf_op jit(solution)/shard_map/reshape | solution.py:71
  6.2 1.1 add_convert_fusion.keep_ref
  7.4 2.2 %collective-permute-done = bf16[320,2,136]{2,0,1:T(8,128)(2,1)S(1)} collective-permute-done((bf16[320,2,136]{2,0,1:T(8,128)(2,1)S(1)}, bf16[320,2,136]{2,0,1:T(8,128)(2,1)S(1)}, u32[]{:S(2)}, u32[]{:S(2)}) %collective-permute-start) | collective-permute-done | bytes 174112 | tf_op jit(solution)/shard_map/ppermute | solution.py:22
  10.0 0.8 copy.144
  10.8 6.2 %shard_map.109 = bf16[2,32,40,256]{3,2,1,0:T(8,128)(2,1)} custom-call(bf16[2,8,40,256]{3,2,1,0:T(8,128)(2,1)} %bitcast.120, bf16[2,8,40,287]{3,2,1,0:T(8,128)(2,1)} %bitcast.119), custom_call_target="tpu_custom_call" | custom-call | tf_op jit(solution)/shard_map/pallas_call | solution.py:73
  17.0 1.5 fusion.33
  18.6 0.5 copy.86
  19.1 1.9 %collective-permute-start.1 = (bf16[40,32,2,4]{0,1,3,2:T(8,128)(2,1)S(1)}, bf16[40,32,2,4]{0,1,3,2:T(8,128)(2,1)S(1)}, u32[]{:S(2)}, u32[]{:S(2)}) collective-permute-start(bf16[40,32,2,4]{0,1,3,2:T(8,128)(2,1)S(1)} %copy.86), channel_id=1, source_target_pairs={{0,1},{1,2},{2,3},{3,4},{4,5},{5,6},{6,7},{8,9},{9,10},{10,11},{11... | collective-permute-start | bytes 61448 | tf_op jit(solution)/shard_map/ppermute | solution.py:22
  21.6 3.6 %collective-permute-start.2 = (bf16[40,32,2,4]{0,1,3,2:T(8,128)(2,1)S(1)}, bf16[40,32,2,4]{0,1,3,2:T(8,128)(2,1)S(1)}, u32[]{:S(2)}, u32[]{:S(2)}) collective-permute-start(bf16[40,32,2,4]{0,1,3,2:T(8,128)(2,1)S(1)} %copy.87), channel_id=1, source_target_pairs={{1,0},{2,1},{3,2},{4,3},{5,4},{6,5},{7,6},{9,8},{10,9},{11,10},{12... | collective-permute-start | bytes 61448 | tf_op jit(solution)/shard_map/ppermute | solution.py:22
  25.8 1.3 collective-permute-done.2
  27.7 1.3 maximum_bitcast_fusion
  29.7 1.2 copy.137
  30.8 4.8 %collective-permute-start.5 = (bf16[40,12288]{1,0:T(8,128)(2,1)}, bf16[40,12288]{1,0:T(8,128)(2,1)}, u32[]{:S(2)}, u32[]{:S(2)}) collective-permute-start(bf16[40,12288]{1,0:T(8,128)(2,1)} %bitcast.67), channel_id=1, source_target_pairs={{8,0},{16,8},{24,16},{32,24},{40,32},{48,40},{56,48},{9,1},{17,9},... | collective-permute-start | bytes 2949128 | tf_op jit(solution)/shard_map/ppermute | solution.py:22
  35.6 1.1 copy.134
  36.7 2.2 %collective-permute-start.3 = (bf16[40,12288]{1,0:T(8,128)(2,1)}, bf16[40,12288]{1,0:T(8,128)(2,1)S(1)}, u32[]{:S(2)}, u32[]{:S(2)}) collective-permute-start(bf16[40,12288]{1,0:T(8,128)(2,1)} %bitcast.55), channel_id=1, source_target_pairs={{0,8},{8,16},{16,24},{24,32},{32,40},{40,48},{48,56},{1,9},{9,17},... | collective-permute-start | bytes 2949128 | tf_op jit(solution)/shard_map/ppermute | solution.py:22
  38.9 0.7 fusion.5
  39.6 0.7 pad_maximum_fusion.1
  40.4 0.8 stack.107
  41.2 1.0 copy.97
  42.2 0.8 stack.109
  43.0 1.0 pad_maximum_fusion
  44.1 0.8 reshape.150.w_ref
  45.6 0.7 copy.98.b_ref
  46.3 1.6 %pad_maximum_fusion.3.w_ref = bf16[2,96,288]{2,1,0:T(8,128)(2,1)} fusion(bf16[1,96,288]{2,1,0:T(8,128)(2,1)} %stack.109, bf16[1,96,288]{2,1,0:T(8,128)(2,1)} %stack.107), kind=kLoop, calls=%fused_computation.17 | loop fusion | flops 55296 | bytes 221184 | tf_op jit(solution)/shard_map/stack | solution.py:152
  48.1 1.2 copy.135
  49.3 1.2 copy.136
  50.5 7.2 %shard_map.110.part_ref = f32[32,24576]{1,0:T(8,128)} custom-call(bf16[48,12288]{1,0:T(8,128)(2,1)} %bitcast.113, bf16[48,12288]{1,0:T(8,128)(2,1)} %bitcast.116, bf16[2,96,288]{2,1,0:T(8,128)(2,1)} %pad_maximum_fusion.3.w_ref), custom_call_target="tpu_custom_call" | custom-call | tf_op jit(solution)/shard_map/pallas_call | solution.py:156
  57.7 2.3 %pad.44.halo_ref = bf16[48,12288]{1,0:T(8,128)(2,1)} pad(bf16[40,12288]{1,0:T(8,128)(2,1)} %collective-permute-done.5, bf16[]{:T(256)} %constant.25.clone.1), padding=0_8x0_0 | pad | bytes 2162690 | tf_op jit(solution)/shard_map/jit(_pad)/pad | solution.py:163
  60.0 4.5 %shard_map.112.x1_ref.rest_0_ = bf16[32,12288]{1,0:T(8,128)(2,1)} custom-call(bf16[48,12288]{1,0:T(8,128)(2,1)} %pad.44.halo_ref, bf16[2,96,144]{2,1,0:T(8,128)(2,1)} %reshape.150.w_ref, f32[32,24576]{1,0:T(8,128)} %shard_map.110.part_ref, f32[4,32,1]{2,1,0:T(8,128)} %copy.98.b_ref, f32[4,24576]{1,0:T(4,128)} %add_convert_fusion.keep_ref), custom_call_target="tpu_custom_call" | custom-call | tf_op jit(solution)/shard_map/pallas_call | solution.py:169
  64.5 1.0 collective-permute-done.3
  65.5 1.1 pad.40.halo_ref
  66.7 4.6 %shard_map.111.x0_ref.rest_0_ = bf16[32,12288]{1,0:T(8,128)(2,1)} custom-call(bf16[48,12288]{1,0:T(8,128)(2,1)} %pad.40.halo_ref, bf16[2,96,144]{2,1,0:T(8,128)(2,1)} %reshape.150.w_ref, f32[32,24576]{1,0:T(8,128)} %shard_map.110.part_ref, f32[4,32,1]{2,1,0:T(8,128)} %copy.98.b_ref, f32[4,24576]{1,0:T(4,128)} %add_convert_fusion.keep_ref), custom_call_target="tpu_custom_call" | custom-call | tf_op jit(solution)/shard_map/pallas_call | solution.py:169
  71.3 2.2 %collective-permute-start.7 = (bf16[32,11520]{1,0:T(8,128)(2,1)S(1)}, bf16[32,11520]{1,0:T(8,128)(2,1)S(1)}, u32[]{:S(2)}, u32[]{:S(2)}) collective-permute-start(bf16[32,11520]{1,0:T(8,128)(2,1)S(1)} %slice.153), channel_id=1, source_target_pairs={{0,8},{8,16},{16,24},{24,32},{32,40},{40,48},{48,56},{1,9},{9,17},... | collective-permute-start | bytes 2211848 | tf_op jit(solution)/shard_map/ppermute | solution.py:22
  73.6 5.9 %collective-permute-start.4 = (bf16[32,11520]{1,0:T(8,128)(2,1)S(1)}, bf16[32,11520]{1,0:T(8,128)(2,1)S(1)}, u32[]{:S(2)}, u32[]{:S(2)}) collective-permute-start(bf16[32,11520]{1,0:T(8,128)(2,1)S(1)} %slice.145), channel_id=1, source_target_pairs={{8,0},{16,8},{24,16},{32,24},{40,32},{48,40},{56,48},{9,1},{17,9},... | collective-permute-start | bytes 2211848 | tf_op jit(solution)/shard_map/ppermute | solution.py:22
  80.3 0.8 reshape.151.w_ref
  81.1 0.6 pad_maximum_fusion.10.w_ref
  81.7 1.0 slice_bitcast_fusion.2
  82.7 5.1 %shard_map.113.part_ref = f32[32,24576]{1,0:T(8,128)} custom-call(bf16[32,12288]{1,0:T(8,128)(2,1)} %shard_map.111.x0_ref.rest_0_, bf16[32,12288]{1,0:T(8,128)(2,1)} %shard_map.112.x1_ref.rest_0_, bf16[2,96,192]{2,1,0:T(8,128)(2,1)} %pad_maximum_fusion.10.w_ref), custom_call_target="tpu_custom_call" | custom-call | tf_op jit(solution)/shard_map/pallas_call | solution.py:156
  87.8 6.1 %collective-permute-done.7 = bf16[32,11520]{1,0:T(8,128)(2,1)S(1)} collective-permute-done((bf16[32,11520]{1,0:T(8,128)(2,1)S(1)}, bf16[32,11520]{1,0:T(8,128)(2,1)S(1)}, u32[]{:S(2)}, u32[]{:S(2)}) %collective-permute-start.7) | collective-permute-done | bytes 737312 | tf_op jit(solution)/shard_map/ppermute | solution.py:22
  94.0 0.9 pad.46.halo_ref
  94.9 4.3 %shard_map.115.x0_ref = bf16[32,12288]{1,0:T(8,128)(2,1)} custom-call(bf16[32,12288]{1,0:T(8,128)(2,1)} %pad.46.halo_ref, bf16[2,96,96]{2,1,0:T(8,128)(2,1)} %reshape.151.w_ref, f32[32,24576]{1,0:T(8,128)} %shard_map.113.part_ref, f32[4,32,1]{2,1,0:T(8,128)} %copy.98.b_ref, f32[4,24576]{1,0:T(4,128)} %add_convert_fusion.keep_ref), custom_call_target="tpu_custom_call" | custom-call | tf_op jit(solution)/shard_map/pallas_call | solution.py:169
  99.3 1.0 pad.43.halo_ref
  100.2 4.4 %shard_map.114.x1_ref = bf16[32,12288]{1,0:T(8,128)(2,1)} custom-call(bf16[32,12288]{1,0:T(8,128)(2,1)} %pad.43.halo_ref, bf16[2,96,96]{2,1,0:T(8,128)(2,1)} %reshape.151.w_ref, f32[32,24576]{1,0:T(8,128)} %shard_map.113.part_ref, f32[4,32,1]{2,1,0:T(8,128)} %copy.98.b_ref, f32[4,24576]{1,0:T(4,128)} %add_convert_fusion.keep_ref), custom_call_target="tpu_custom_call" | custom-call | tf_op jit(solution)/shard_map/pallas_call | solution.py:169
  104.7 3.6 %collective-permute-start.8 = (bf16[32,10752]{1,0:T(8,128)(2,1)S(1)}, bf16[32,10752]{1,0:T(8,128)(2,1)S(1)}, u32[]{:S(2)}, u32[]{:S(2)}) collective-permute-start(bf16[32,10752]{1,0:T(8,128)(2,1)S(1)} %slice.155), channel_id=1, source_target_pairs={{8,0},{16,8},{24,16},{32,24},{40,32},{48,40},{56,48},{9,1},{17,9},... | collective-permute-start | bytes 2064392 | tf_op jit(solution)/shard_map/ppermute | solution.py:22
  108.3 1.1 slice.150
  109.5 2.5 %collective-permute-start.6 = (bf16[32,10752]{1,0:T(8,128)(2,1)S(1)}, bf16[32,10752]{1,0:T(8,128)(2,1)S(1)}, u32[]{:S(2)}, u32[]{:S(2)}) collective-permute-start(bf16[32,10752]{1,0:T(8,128)(2,1)S(1)} %slice.150), channel_id=1, source_target_pairs={{0,8},{8,16},{16,24},{24,32},{32,40},{40,48},{48,56},{1,9},{9,17},... | collective-permute-start | bytes 2064392 | tf_op jit(solution)/shard_map/ppermute | solution.py:22
  112.7 0.8 reshape.152.w_ref
  114.2 0.6 pad_maximum_fusion.14.w_ref
  114.8 0.7 pad_maximum_fusion.11.w_ref
  115.5 5.1 %shard_map.116.part_ref = f32[32,24576]{1,0:T(8,128)} custom-call(bf16[32,12288]{1,0:T(8,128)(2,1)} %shard_map.115.x0_ref, bf16[32,12288]{1,0:T(8,128)(2,1)} %shard_map.114.x1_ref, bf16[2,96,192]{2,1,0:T(8,128)(2,1)} %pad_maximum_fusion.11.w_ref), custom_call_target="tpu_custom_call" | custom-call | tf_op jit(solution)/shard_map/pallas_call | solution.py:156
  120.6 2.6 %collective-permute-done.8 = bf16[32,10752]{1,0:T(8,128)(2,1)S(1)} collective-permute-done((bf16[32,10752]{1,0:T(8,128)(2,1)S(1)}, bf16[32,10752]{1,0:T(8,128)(2,1)S(1)}, u32[]{:S(2)}, u32[]{:S(2)}) %collective-permute-start.8) | collective-permute-done | bytes 688160 | tf_op jit(solution)/shard_map/ppermute | solution.py:22
  123.2 0.9 pad.47.halo_ref
  124.2 4.9 %shard_map.118.x1_ref = bf16[32,12288]{1,0:T(8,128)(2,1)} custom-call(bf16[32,12288]{1,0:T(8,128)(2,1)} %pad.47.halo_ref, bf16[2,96,96]{2,1,0:T(8,128)(2,1)} %reshape.152.w_ref, f32[32,24576]{1,0:T(8,128)} %shard_map.116.part_ref, f32[4,32,1]{2,1,0:T(8,128)} %copy.98.b_ref, f32[4,24576]{1,0:T(4,128)} %add_convert_fusion.keep_ref, ...), custom_call_target="tpu_custom_call" | custom-call | tf_op jit(solution)/shard_map/pallas_call | solution.py:169
  129.0 1.0 collective-permute-done.6
  130.0 1.0 pad.45.halo_ref
  131.0 4.9 %shard_map.117.x0_ref = bf16[32,12288]{1,0:T(8,128)(2,1)} custom-call(bf16[32,12288]{1,0:T(8,128)(2,1)} %pad.45.halo_ref, bf16[2,96,96]{2,1,0:T(8,128)(2,1)} %reshape.152.w_ref, f32[32,24576]{1,0:T(8,128)} %shard_map.116.part_ref, f32[4,32,1]{2,1,0:T(8,128)} %copy.98.b_ref, f32[4,24576]{1,0:T(4,128)} %add_convert_fusion.keep_ref, ...), custom_call_target="tpu_custom_call" | custom-call | tf_op jit(solution)/shard_map/pallas_call | solution.py:169
  135.8 6.7 %shard_map.119 = f32[8,49152]{1,0:T(8,128)} custom-call(bf16[32,12288]{1,0:T(8,128)(2,1)} %shard_map.117.x0_ref, bf16[32,12288]{1,0:T(8,128)(2,1)} %shard_map.118.x1_ref, bf16[4,24,192]{2,1,0:T(8,128)(2,1)} %pad_maximum_fusion.14.w_ref), custom_call_target="tpu_custom_call" | custom-call | tf_op jit(solution)/shard_map/pallas_call | solution.py:258
  142.5 1.9 %slice_reduce_fusion = f32[49152]{0:T(1024)S(1)} fusion(f32[8,49152]{1,0:T(8,128)} %shard_map.119), kind=kLoop, calls=%fused_computation.10 | loop fusion | bytes 393216 | tf_op jit(solution)/shard_map/slice | solution.py:262
  144.5 4.9 %collective-permute-start.10 = (f32[24,256]{1,0:T(8,128)S(1)}, f32[24,256]{1,0:T(8,128)S(1)}, u32[]{:S(2)}, u32[]{:S(2)}) collective-permute-start(f32[24,256]{1,0:T(8,128)S(1)} %get-tuple-element.29), channel_id=1, source_target_pairs={{8,0},{16,8},{24,16},{32,24},{40,32},{48,40},{56,48},{9,1},{17,9},... | collective-permute-start | bytes 73736 | tf_op jit(solution)/shard_map/ppermute | solution.py:22
  149.4 1.9 %collective-permute-start.9 = (f32[24,256]{1,0:T(8,128)S(1)}, f32[24,256]{1,0:T(8,128)S(1)}, u32[]{:S(2)}, u32[]{:S(2)}) collective-permute-start(f32[24,256]{1,0:T(8,128)S(1)} %get-tuple-element.28), channel_id=1, source_target_pairs={{0,8},{8,16},{16,24},{24,32},{32,40},{40,48},{48,56},{1,9},{9,17},... | collective-permute-start | bytes 73736 | tf_op jit(solution)/shard_map/ppermute | solution.py:22
  151.4 5.9 %collective-permute-done.9 = f32[24,256]{1,0:T(8,128)S(1)} collective-permute-done((f32[24,256]{1,0:T(8,128)S(1)}, f32[24,256]{1,0:T(8,128)S(1)}, u32[]{:S(2)}, u32[]{:S(2)}) %collective-permute-start.9) | collective-permute-done | bytes 24608 | tf_op jit(solution)/shard_map/ppermute | solution.py:22
  157.3 0.7 fusion.4
  (91 shorter events, 6.5 us)
Async XLA Ops:
  1.2 8.4 %collective-permute-start = (bf16[320,2,136]{2,0,1:T(8,128)(2,1)S(1)}, bf16[320,2,136]{2,0,1:T(8,128)(2,1)S(1)}, u32[]{:S(2)}, u32[]{:S(2)}) collective-permute-start(bf16[320,2,136]{2,0,1:T(8,128)(2,1)S(1)} %slice.139), channel_id=1, source_target_pairs={{0,1},{1,2},{2,3},{3,4},{4,5},{5,6},{6,7},{8,9},{9,10},{10,11},{11... | collective-permute-start | bytes 522248 | tf_op jit(solution)/shard_map/ppermute | solution.py:22
  18.6 9.1 %copy-start.2 = (bf16[2,32,40,256]{3,2,1,0:T(8,128)(2,1)S(1)}, bf16[2,32,40,256]{3,2,1,0:T(8,128)(2,1)}, u32[]{:S(2)}) copy-start(bf16[2,32,40,256]{3,2,1,0:T(8,128)(2,1)} %shard_map.109) | copy-start | bytes 3932164
  19.1 6.2 %collective-permute-start.1 = (bf16[40,32,2,4]{0,1,3,2:T(8,128)(2,1)S(1)}, bf16[40,32,2,4]{0,1,3,2:T(8,128)(2,1)S(1)}, u32[]{:S(2)}, u32[]{:S(2)}) collective-permute-start(bf16[40,32,2,4]{0,1,3,2:T(8,128)(2,1)S(1)} %copy.86), channel_id=1, source_target_pairs={{0,1},{1,2},{2,3},{3,4},{4,5},{5,6},{6,7},{8,9},{9,10},{10,11},{11... | collective-permute-start | bytes 61448 | tf_op jit(solution)/shard_map/ppermute | solution.py:22
  21.6 5.5 %collective-permute-start.2 = (bf16[40,32,2,4]{0,1,3,2:T(8,128)(2,1)S(1)}, bf16[40,32,2,4]{0,1,3,2:T(8,128)(2,1)S(1)}, u32[]{:S(2)}, u32[]{:S(2)}) collective-permute-start(bf16[40,32,2,4]{0,1,3,2:T(8,128)(2,1)S(1)} %copy.87), channel_id=1, source_target_pairs={{1,0},{2,1},{3,2},{4,3},{5,4},{6,5},{7,6},{9,8},{10,9},{11,10},{12... | collective-permute-start | bytes 61448 | tf_op jit(solution)/shard_map/ppermute | solution.py:22
  29.6 9.2 %copy-start.4 = (bf16[32,40,3,3,3]{1,0,4,3,2:T(8,128)(2,1)S(1)}, bf16[32,40,3,3,3]{1,0,4,3,2:T(8,128)(2,1)}, u32[]{:S(2)}) copy-start(bf16[32,40,3,3,3]{1,0,4,3,2:T(8,128)(2,1)} %param.14) | copy-start | bytes 207364
  30.8 26.8 %collective-permute-start.5 = (bf16[40,12288]{1,0:T(8,128)(2,1)}, bf16[40,12288]{1,0:T(8,128)(2,1)}, u32[]{:S(2)}, u32[]{:S(2)}) collective-permute-start(bf16[40,12288]{1,0:T(8,128)(2,1)} %bitcast.67), channel_id=1, source_target_pairs={{8,0},{16,8},{24,16},{32,24},{40,32},{48,40},{56,48},{9,1},{17,9},... | collective-permute-start | bytes 2949128 | tf_op jit(solution)/shard_map/ppermute | solution.py:22
  36.7 8.9 %copy-start.7 = (f32[32]{0:T(128)S(1)}, f32[32]{0:T(128)}, u32[]{:S(2)}) copy-start(f32[32]{0:T(128)} %param.19) | copy-start | bytes 388
  36.7 8.9 %copy-start.8 = (f32[32]{0:T(128)S(1)}, f32[32]{0:T(128)}, u32[]{:S(2)}) copy-start(f32[32]{0:T(128)} %param.17) | copy-start | bytes 388
  36.7 8.9 %copy-start.9 = (f32[32]{0:T(128)S(1)}, f32[32]{0:T(128)}, u32[]{:S(2)}) copy-start(f32[32]{0:T(128)} %param.15) | copy-start | bytes 388
  36.7 28.9 %collective-permute-start.3 = (bf16[40,12288]{1,0:T(8,128)(2,1)}, bf16[40,12288]{1,0:T(8,128)(2,1)S(1)}, u32[]{:S(2)}, u32[]{:S(2)}) collective-permute-start(bf16[40,12288]{1,0:T(8,128)(2,1)} %bitcast.55), channel_id=1, source_target_pairs={{0,8},{8,16},{16,24},{24,32},{32,40},{40,48},{48,56},{1,9},{9,17},... | collective-permute-start | bytes 2949128 | tf_op jit(solution)/shard_map/ppermute | solution.py:22
  66.6 4.6 %copy-start.1 = (bf16[32,12288]{1,0:T(8,128)(2,1)S(1)}, bf16[32,12288]{1,0:T(8,128)(2,1)}, u32[]{:S(2)}) copy-start(bf16[32,12288]{1,0:T(8,128)(2,1)} %shard_map.112.x1_ref.rest_0_) | copy-start | bytes 2359300
  71.3 2.3 %copy-start = (bf16[32,12288]{1,0:T(8,128)(2,1)S(1)}, bf16[32,12288]{1,0:T(8,128)(2,1)}, u32[]{:S(2)}) copy-start(bf16[32,12288]{1,0:T(8,128)(2,1)} %shard_map.111.x0_ref.rest_0_) | copy-start | bytes 2359300
  71.3 8.2 %copy-start.5 = (bf16[32,32,3,3,3]{1,0,4,3,2:T(8,128)(2,1)S(1)}, bf16[32,32,3,3,3]{1,0,4,3,2:T(8,128)(2,1)}, u32[]{:S(2)}) copy-start(bf16[32,32,3,3,3]{1,0,4,3,2:T(8,128)(2,1)} %param.16) | copy-start | bytes 165892
  71.3 22.6 %collective-permute-start.7 = (bf16[32,11520]{1,0:T(8,128)(2,1)S(1)}, bf16[32,11520]{1,0:T(8,128)(2,1)S(1)}, u32[]{:S(2)}, u32[]{:S(2)}) collective-permute-start(bf16[32,11520]{1,0:T(8,128)(2,1)S(1)} %slice.153), channel_id=1, source_target_pairs={{0,8},{8,16},{16,24},{24,32},{32,40},{40,48},{48,56},{1,9},{9,17},... | collective-permute-start | bytes 2211848 | tf_op jit(solution)/shard_map/ppermute | solution.py:22
  73.6 25.7 %collective-permute-start.4 = (bf16[32,11520]{1,0:T(8,128)(2,1)S(1)}, bf16[32,11520]{1,0:T(8,128)(2,1)S(1)}, u32[]{:S(2)}, u32[]{:S(2)}) collective-permute-start(bf16[32,11520]{1,0:T(8,128)(2,1)S(1)} %slice.145), channel_id=1, source_target_pairs={{8,0},{16,8},{24,16},{32,24},{40,32},{48,40},{56,48},{9,1},{17,9},... | collective-permute-start | bytes 2211848 | tf_op jit(solution)/shard_map/ppermute | solution.py:22
  100.2 4.4 %copy-start.3 = (bf16[32,12288]{1,0:T(8,128)(2,1)S(1)}, bf16[32,12288]{1,0:T(8,128)(2,1)}, u32[]{:S(2)}) copy-start(bf16[32,12288]{1,0:T(8,128)(2,1)} %shard_map.115.x0_ref) | copy-start | bytes 2359300
  104.7 8.8 %copy-start.6 = (bf16[1,32,3,3,3]{1,4,3,2,0:T(4,128)(2,1)S(1)}, bf16[1,32,3,3,3]{1,4,3,2,0:T(4,128)(2,1)}, u32[]{:S(2)}) copy-start(bf16[1,32,3,3,3]{1,4,3,2,0:T(4,128)(2,1)} %param.20) | copy-start | bytes 5188
  104.7 18.5 %collective-permute-start.8 = (bf16[32,10752]{1,0:T(8,128)(2,1)S(1)}, bf16[32,10752]{1,0:T(8,128)(2,1)S(1)}, u32[]{:S(2)}, u32[]{:S(2)}) collective-permute-start(bf16[32,10752]{1,0:T(8,128)(2,1)S(1)} %slice.155), channel_id=1, source_target_pairs={{8,0},{16,8},{24,16},{32,24},{40,32},{48,40},{56,48},{9,1},{17,9},... | collective-permute-start | bytes 2064392 | tf_op jit(solution)/shard_map/ppermute | solution.py:22
  109.5 20.5 %collective-permute-start.6 = (bf16[32,10752]{1,0:T(8,128)(2,1)S(1)}, bf16[32,10752]{1,0:T(8,128)(2,1)S(1)}, u32[]{:S(2)}, u32[]{:S(2)}) collective-permute-start(bf16[32,10752]{1,0:T(8,128)(2,1)S(1)} %slice.150), channel_id=1, source_target_pairs={{0,8},{8,16},{16,24},{24,32},{32,40},{40,48},{48,56},{1,9},{9,17},... | collective-permute-start | bytes 2064392 | tf_op jit(solution)/shard_map/ppermute | solution.py:22
  144.5 6.9 %collective-permute-start.10 = (f32[24,256]{1,0:T(8,128)S(1)}, f32[24,256]{1,0:T(8,128)S(1)}, u32[]{:S(2)}, u32[]{:S(2)}) collective-permute-start(f32[24,256]{1,0:T(8,128)S(1)} %get-tuple-element.29), channel_id=1, source_target_pairs={{8,0},{16,8},{24,16},{32,24},{40,32},{48,40},{56,48},{9,1},{17,9},... | collective-permute-start | bytes 73736 | tf_op jit(solution)/shard_map/ppermute | solution.py:22
  149.4 7.8 %collective-permute-start.9 = (f32[24,256]{1,0:T(8,128)S(1)}, f32[24,256]{1,0:T(8,128)S(1)}, u32[]{:S(2)}, u32[]{:S(2)}) collective-permute-start(f32[24,256]{1,0:T(8,128)S(1)} %get-tuple-element.28), channel_id=1, source_target_pairs={{0,8},{8,16},{16,24},{24,32},{32,40},{40,48},{48,56},{1,9},{9,17},... | collective-permute-start | bytes 73736 | tf_op jit(solution)/shard_map/ppermute | solution.py:22

commit v2 on v0

--- a/solution.py
+++ b/solution.py
@@ -212,7 +212,7 @@
     )
     count_cols = width + 2 * EXT
     corr = jnp.transpose(corr, (0, 2, 1, 3))
-    chans_in = -(-G // 16) * 16
+    chans_in = G
     corr = jnp.pad(
         corr, ((0, chans_in - G), (0, 0), (0, DEPTH - count), (0, LINE - count_cols))
     )

time: 158 us -> 158 us (level)
  waiting for transfers between devices: 29.9 us -> 32.9 us
  Pallas kernels: 49.9 us -> 48 us
    ppermute x11, waiting for transfers between devices: 29.9 us -> 32.9 us  [from_behind(): return lax.ppermute(array, axis, pairs)]
    pallas_call x3, Pallas kernels: 17.6 us -> 15.8 us  [conv_layer(): pl.pallas_call(functools.partial(own_kernel, cout=rows_out), out_shape=ja...]
  transfers between devices with their start and end apart: 11 -> 11, of which waited for: 9 -> 9; matrix products, arithmetic and copies ran while one was open for 11% -> 10% of each run, Pallas kernels for 11% -> 10%
where the time goes in v2:
time: 158 us; the launch traced here: 157 us
  Pallas kernels  48 us (30%)
  starting transfers between devices  41.2 us (26%)
  waiting for transfers between devices  32.9 us (21%)
  local copies, waits for them, and re-layouts  25.8 us (16%)
  other arithmetic  7.33 us (5%)
  between operations  1.89 us (1%)
    ppermute x11, starting transfers between devices, from_behind(): return lax.ppermute(array, axis, pairs)  41.2 us
    ppermute x11, waiting for transfers between devices, from_behind(): return lax.ppermute(array, axis, pairs)  32.9 us
    pallas_call x3, Pallas kernels, conv_layer(): pl.pallas_call(functools.partial(halo_kernel, cout=rows_out, relu=relu, i...  19.2 us
    pallas_call x3, Pallas kernels, conv_layer(): pl.pallas_call(functools.partial(own_kernel, cout=rows_out), out_shape=ja...  15.8 us
    pallas_call x1, Pallas kernels, cost_head(): pl.pallas_call(functools.partial(own_kernel, cout=rows_out), out_shape=ja...  6.83 us
    pallas_call x1, Pallas kernels, correlate(): pl.pallas_call(correlate_kernel, out_shape=jax.ShapeDtypeStruct((rows, co...  6.2 us
    slice x3, local copies, waits for them, and re-layouts, conv_layer(): below = jnp.pad(from_behind(own[:sent, :span], 'row', -1), pad)  3.98 us
  transfers between devices with their start and end apart: 11, of which 9 were waited for; matrix products, arithmetic and copies ran while one was open for 10% of the time, Pallas kernels for 10%

profile of v2, /device:TPU:100, one launch (start us, length us, event | category | flops | bytes accessed | tf_op | source)
XLA Modules:
  0.0 157.2 jit_solution(6623924435544616632)
XLA Ops:
  0.0 1.0 copy.71
  1.0 0.2 slice.121
  1.2 1.9 %collective-permute-start = (bf16[320,2,136]{2,0,1:T(8,128)(2,1)S(1)}, bf16[320,2,136]{2,0,1:T(8,128)(2,1)S(1)}, u32[]{:S(2)}, u32[]{:S(2)}) collective-permute-start(bf16[320,2,136]{2,0,1:T(8,128)(2,1)S(1)} %slice.121), channel_id=1, source_target_pairs={{0,1},{1,2},{2,3},{3,4},{4,5},{5,6},{6,7},{8,9},{9,10},{10,11},{11... | collective-permute-start | bytes 522248 | tf_op jit(solution)/shard_map/ppermute | solution.py:22
  3.8 1.8 %copy.121 = bf16[40,8,2,256]{3,0,1,2:T(8,128)(2,1)} copy(bf16[40,8,2,256]{3,2,1,0:T(2,128)(2,1)} %bitcast.102) | data formatting | bytes 655360 | tf_op jit(solution)/shard_map/reshape | solution.py:71
  6.0 3.6 %collective-permute-done = bf16[320,2,136]{2,0,1:T(8,128)(2,1)S(1)} collective-permute-done((bf16[320,2,136]{2,0,1:T(8,128)(2,1)S(1)}, bf16[320,2,136]{2,0,1:T(8,128)(2,1)S(1)}, u32[]{:S(2)}, u32[]{:S(2)}) %collective-permute-start) | collective-permute-done | bytes 174112 | tf_op jit(solution)/shard_map/ppermute | solution.py:22
  9.6 0.4 fusion.2
  10.0 0.9 copy.120
  10.8 6.2 %shard_map.109 = bf16[2,32,40,256]{3,2,1,0:T(8,128)(2,1)} custom-call(bf16[2,8,40,256]{3,2,1,0:T(8,128)(2,1)} %bitcast.101, bf16[2,8,40,287]{3,2,1,0:T(8,128)(2,1)} %bitcast.100), custom_call_target="tpu_custom_call" | custom-call | tf_op jit(solution)/shard_map/pallas_call | solution.py:73
  17.0 1.5 fusion.29
  18.6 0.5 copy.74
  19.1 1.9 %collective-permute-start.1 = (bf16[40,32,2,4]{0,1,3,2:T(8,128)(2,1)S(1)}, bf16[40,32,2,4]{0,1,3,2:T(8,128)(2,1)S(1)}, u32[]{:S(2)}, u32[]{:S(2)}) collective-permute-start(bf16[40,32,2,4]{0,1,3,2:T(8,128)(2,1)S(1)} %copy.74), channel_id=1, source_target_pairs={{0,1},{1,2},{2,3},{3,4},{4,5},{5,6},{6,7},{8,9},{9,10},{10,11},{11... | collective-permute-start | bytes 61448 | tf_op jit(solution)/shard_map/ppermute | solution.py:22
  21.1 0.5 copy.75
  21.6 3.6 %collective-permute-start.2 = (bf16[40,32,2,4]{0,1,3,2:T(8,128)(2,1)S(1)}, bf16[40,32,2,4]{0,1,3,2:T(8,128)(2,1)S(1)}, u32[]{:S(2)}, u32[]{:S(2)}) collective-permute-start(bf16[40,32,2,4]{0,1,3,2:T(8,128)(2,1)S(1)} %copy.75), channel_id=1, source_target_pairs={{1,0},{2,1},{3,2},{4,3},{5,4},{6,5},{7,6},{9,8},{10,9},{11,10},{12... | collective-permute-start | bytes 61448 | tf_op jit(solution)/shard_map/ppermute | solution.py:22
  25.6 0.5 copy.76
  26.1 1.0 collective-permute-done.2
  27.2 0.5 copy.77
  27.7 1.3 maximum_bitcast_fusion
  28.9 0.5 pad_select_fusion
  29.4 0.2 copy.116
  29.7 1.1 fusion.26
  30.8 0.5 copy-done
  31.3 3.6 %collective-permute-start.3 = (bf16[40,12288]{1,0:T(8,128)(2,1)}, bf16[40,12288]{1,0:T(8,128)(2,1)S(1)}, u32[]{:S(2)}, u32[]{:S(2)}) collective-permute-start(bf16[40,12288]{1,0:T(8,128)(2,1)} %get-tuple-element.6), channel_id=1, source_target_pairs={{0,8},{8,16},{16,24},{24,32},{32,40},{40,48},{48,56},{1,9},{9,17},... | collective-permute-start | bytes 2949128 | tf_op jit(solution)/shard_map/ppermute | solution.py:22
  34.9 4.6 %collective-permute-start.4 = (bf16[40,12288]{1,0:T(8,128)(2,1)S(1)}, bf16[40,12288]{1,0:T(8,128)(2,1)S(1)}, u32[]{:S(2)}, u32[]{:S(2)}) collective-permute-start(bf16[40,12288]{1,0:T(8,128)(2,1)S(1)} %get-tuple-element.5), channel_id=1, source_target_pairs={{8,0},{16,8},{24,16},{32,24},{40,32},{48,40},{56,48},{9,1},{17,9},... | collective-permute-start | bytes 2949128 | tf_op jit(solution)/shard_map/ppermute | solution.py:22
  39.6 1.2 add_convert_fusion.keep_ref
  41.5 0.8 reshape.152.w_ref
  43.0 0.7 copy.84.b_ref
  43.7 0.7 pad_maximum_fusion.9.w_ref
  44.4 5.5 %shard_map.110.part_ref = f32[32,24576]{1,0:T(8,128)} custom-call(bf16[40,24576]{1,0:T(8,128)(2,1)} %bitcast.96, bf16[2,96,240]{2,1,0:T(8,128)(2,1)} %pad_maximum_fusion.9.w_ref), custom_call_target="tpu_custom_call" | custom-call | tf_op jit(solution)/shard_map/pallas_call | solution.py:158
  49.9 10.0 %collective-permute-done.3.above_ref = bf16[40,12288]{1,0:T(8,128)(2,1)S(1)} collective-permute-done((bf16[40,12288]{1,0:T(8,128)(2,1)}, bf16[40,12288]{1,0:T(8,128)(2,1)S(1)}, u32[]{:S(2)}, u32[]{:S(2)}) %collective-permute-start.3) | collective-permute-done | bytes 983072 | tf_op jit(solution)/shard_map/ppermute | solution.py:22
  59.9 1.5 collective-permute-done.4.below_ref
  61.4 1.0 copy-done.3
  62.4 6.1 %shard_map.111.x_ref.rest_0_ = bf16[32,24576]{1,0:T(8,128)(2,1)} custom-call(bf16[40,12288]{1,0:T(8,128)(2,1)} %copy-done.2, bf16[40,12288]{1,0:T(8,128)(2,1)} %copy-done.3, bf16[2,96,120]{2,1,0:T(8,128)(2,1)} %reshape.152.w_ref, f32[32,24576]{1,0:T(8,128)} %shard_map.110.part_ref, f32[4,32,1]{2,1,0:T(8,128)} %copy.84.b_ref, f32[4,24576]{1,0:T(4,128)} %add_convert_fusion.keep_ref), custom_call_target="tpu_custom_call" | custom-call | tf_op jit(solution)/shard_map/pallas_call | solution.py:169
  68.4 1.5 fusion.28
  69.9 3.4 %collective-permute-start.5 = (bf16[32,11520]{1,0:T(8,128)(2,1)S(1)}, bf16[32,11520]{1,0:T(8,128)(2,1)S(1)}, u32[]{:S(2)}, u32[]{:S(2)}) collective-permute-start(bf16[32,11520]{1,0:T(8,128)(2,1)S(1)} %get-tuple-element.10), channel_id=1, source_target_pairs={{0,8},{8,16},{16,24},{24,32},{32,40},{40,48},{48,56},{1,9},{9,17},... | collective-permute-start | bytes 2211848 | tf_op jit(solution)/shard_map/ppermute | solution.py:22
  73.3 5.0 %collective-permute-start.6 = (bf16[32,11520]{1,0:T(8,128)(2,1)S(1)}, bf16[32,11520]{1,0:T(8,128)(2,1)S(1)}, u32[]{:S(2)}, u32[]{:S(2)}) collective-permute-start(bf16[32,11520]{1,0:T(8,128)(2,1)S(1)} %get-tuple-element.9), channel_id=1, source_target_pairs={{8,0},{16,8},{24,16},{32,24},{40,32},{48,40},{56,48},{9,1},{17,9},... | collective-permute-start | bytes 2211848 | tf_op jit(solution)/shard_map/ppermute | solution.py:22
  78.6 0.1 stack.118
  78.9 0.1 stack.120
  79.2 0.8 reshape.153.w_ref
  79.9 0.6 pad_maximum_fusion.10.w_ref
  80.6 1.0 slice_bitcast_fusion.3
  81.6 5.1 %shard_map.112.part_ref = f32[32,24576]{1,0:T(8,128)} custom-call(bf16[32,24576]{1,0:T(8,128)(2,1)} %shard_map.111.x_ref.rest_0_, bf16[2,96,192]{2,1,0:T(8,128)(2,1)} %pad_maximum_fusion.10.w_ref), custom_call_target="tpu_custom_call" | custom-call | tf_op jit(solution)/shard_map/pallas_call | solution.py:158
  86.7 6.5 %collective-permute-done.5 = bf16[32,11520]{1,0:T(8,128)(2,1)S(1)} collective-permute-done((bf16[32,11520]{1,0:T(8,128)(2,1)S(1)}, bf16[32,11520]{1,0:T(8,128)(2,1)S(1)}, u32[]{:S(2)}, u32[]{:S(2)}) %collective-permute-start.5) | collective-permute-done | bytes 737312 | tf_op jit(solution)/shard_map/ppermute | solution.py:22
  93.2 0.9 pad.30.above_ref
  94.1 0.2 collective-permute-done.6
  94.4 0.9 pad.31.below_ref
  95.3 5.9 %shard_map.113.x_ref = bf16[32,24576]{1,0:T(8,128)(2,1)} custom-call(bf16[32,12288]{1,0:T(8,128)(2,1)} %pad.30.above_ref, bf16[32,12288]{1,0:T(8,128)(2,1)} %pad.31.below_ref, bf16[2,96,96]{2,1,0:T(8,128)(2,1)} %reshape.153.w_ref, f32[32,24576]{1,0:T(8,128)} %shard_map.112.part_ref, f32[4,32,1]{2,1,0:T(8,128)} %copy.84.b_ref, ...), custom_call_target="tpu_custom_call" | custom-call | tf_op jit(solution)/shard_map/pallas_call | solution.py:169
  101.3 1.4 fusion.27
  102.7 2.3 %collective-permute-start.7 = (bf16[32,10752]{1,0:T(8,128)(2,1)S(1)}, bf16[32,10752]{1,0:T(8,128)(2,1)S(1)}, u32[]{:S(2)}, u32[]{:S(2)}) collective-permute-start(bf16[32,10752]{1,0:T(8,128)(2,1)S(1)} %get-tuple-element.8), channel_id=1, source_target_pairs={{0,8},{8,16},{16,24},{24,32},{32,40},{40,48},{48,56},{1,9},{9,17},... | collective-permute-start | bytes 2064392 | tf_op jit(solution)/shard_map/ppermute | solution.py:22
  105.0 6.4 %collective-permute-start.8 = (bf16[32,10752]{1,0:T(8,128)(2,1)S(1)}, bf16[32,10752]{1,0:T(8,128)(2,1)S(1)}, u32[]{:S(2)}, u32[]{:S(2)}) collective-permute-start(bf16[32,10752]{1,0:T(8,128)(2,1)S(1)} %get-tuple-element.7), channel_id=1, source_target_pairs={{8,0},{16,8},{24,16},{32,24},{40,32},{48,40},{56,48},{9,1},{17,9},... | collective-permute-start | bytes 2064392 | tf_op jit(solution)/shard_map/ppermute | solution.py:22
  112.1 0.8 reshape.154.w_ref
  113.6 0.6 pad_maximum_fusion.14.w_ref
  114.2 0.7 pad_maximum_fusion.11.w_ref
  114.9 5.1 %shard_map.114.part_ref = f32[32,24576]{1,0:T(8,128)} custom-call(bf16[32,24576]{1,0:T(8,128)(2,1)} %shard_map.113.x_ref, bf16[2,96,192]{2,1,0:T(8,128)(2,1)} %pad_maximum_fusion.11.w_ref), custom_call_target="tpu_custom_call" | custom-call | tf_op jit(solution)/shard_map/pallas_call | solution.py:158
  120.0 4.0 %collective-permute-done.7 = bf16[32,10752]{1,0:T(8,128)(2,1)S(1)} collective-permute-done((bf16[32,10752]{1,0:T(8,128)(2,1)S(1)}, bf16[32,10752]{1,0:T(8,128)(2,1)S(1)}, u32[]{:S(2)}, u32[]{:S(2)}) %collective-permute-start.7) | collective-permute-done | bytes 688160 | tf_op jit(solution)/shard_map/ppermute | solution.py:22
  124.0 0.9 pad.32.above_ref
  124.9 0.2 collective-permute-done.8
  125.2 0.9 pad.33.below_ref
  126.1 7.2 %shard_map.115.x_ref = bf16[32,24576]{1,0:T(8,128)(2,1)} custom-call(bf16[32,12288]{1,0:T(8,128)(2,1)} %pad.32.above_ref, bf16[32,12288]{1,0:T(8,128)(2,1)} %pad.33.below_ref, bf16[2,96,96]{2,1,0:T(8,128)(2,1)} %reshape.154.w_ref, f32[32,24576]{1,0:T(8,128)} %shard_map.114.part_ref, f32[4,32,1]{2,1,0:T(8,128)} %copy.84.b_ref, ...), custom_call_target="tpu_custom_call" | custom-call | tf_op jit(solution)/shard_map/pallas_call | solution.py:169
  133.3 6.8 %shard_map.116 = f32[8,49152]{1,0:T(8,128)} custom-call(bf16[32,24576]{1,0:T(8,128)(2,1)} %shard_map.115.x_ref, bf16[4,24,192]{2,1,0:T(8,128)(2,1)} %pad_maximum_fusion.14.w_ref), custom_call_target="tpu_custom_call" | custom-call | tf_op jit(solution)/shard_map/pallas_call | solution.py:257
  140.1 1.9 %slice_reduce_fusion = f32[49152]{0:T(1024)S(1)} fusion(f32[8,49152]{1,0:T(8,128)} %shard_map.116), kind=kLoop, calls=%fused_computation.10 | loop fusion | bytes 393216 | tf_op jit(solution)/shard_map/slice | solution.py:261
  142.1 6.5 %collective-permute-start.10 = (f32[24,256]{1,0:T(8,128)S(1)}, f32[24,256]{1,0:T(8,128)S(1)}, u32[]{:S(2)}, u32[]{:S(2)}) collective-permute-start(f32[24,256]{1,0:T(8,128)S(1)} %get-tuple-element.31), channel_id=1, source_target_pairs={{8,0},{16,8},{24,16},{32,24},{40,32},{48,40},{56,48},{9,1},{17,9},... | collective-permute-start | bytes 73736 | tf_op jit(solution)/shard_map/ppermute | solution.py:22
  148.6 1.9 %collective-permute-start.9 = (f32[24,256]{1,0:T(8,128)S(1)}, f32[24,256]{1,0:T(8,128)S(1)}, u32[]{:S(2)}, u32[]{:S(2)}) collective-permute-start(f32[24,256]{1,0:T(8,128)S(1)} %get-tuple-element.30), channel_id=1, source_target_pairs={{0,8},{8,16},{16,24},{24,32},{32,40},{40,48},{48,56},{1,9},{9,17},... | collective-permute-start | bytes 73736 | tf_op jit(solution)/shard_map/ppermute | solution.py:22
  150.5 5.9 %collective-permute-done.9 = f32[24,256]{1,0:T(8,128)S(1)} collective-permute-done((f32[24,256]{1,0:T(8,128)S(1)}, f32[24,256]{1,0:T(8,128)S(1)}, u32[]{:S(2)}, u32[]{:S(2)}) %collective-permute-start.9) | collective-permute-done | bytes 24608 | tf_op jit(solution)/shard_map/ppermute | solution.py:22
  156.5 0.7 fusion.3
  (80 shorter events, 3.5 us)
Async XLA Ops:
  1.2 8.4 %collective-permute-start = (bf16[320,2,136]{2,0,1:T(8,128)(2,1)S(1)}, bf16[320,2,136]{2,0,1:T(8,128)(2,1)S(1)}, u32[]{:S(2)}, u32[]{:S(2)}) collective-permute-start(bf16[320,2,136]{2,0,1:T(8,128)(2,1)S(1)} %slice.121), channel_id=1, source_target_pairs={{0,1},{1,2},{2,3},{3,4},{4,5},{5,6},{6,7},{8,9},{9,10},{10,11},{11... | collective-permute-start | bytes 522248 | tf_op jit(solution)/shard_map/ppermute | solution.py:22
  18.6 9.1 %copy-start.1 = (bf16[2,32,40,256]{3,2,1,0:T(8,128)(2,1)S(1)}, bf16[2,32,40,256]{3,2,1,0:T(8,128)(2,1)}, u32[]{:S(2)}) copy-start(bf16[2,32,40,256]{3,2,1,0:T(8,128)(2,1)} %shard_map.109) | copy-start | bytes 3932164
  19.1 6.5 %collective-permute-start.1 = (bf16[40,32,2,4]{0,1,3,2:T(8,128)(2,1)S(1)}, bf16[40,32,2,4]{0,1,3,2:T(8,128)(2,1)S(1)}, u32[]{:S(2)}, u32[]{:S(2)}) collective-permute-start(bf16[40,32,2,4]{0,1,3,2:T(8,128)(2,1)S(1)} %copy.74), channel_id=1, source_target_pairs={{0,1},{1,2},{2,3},{3,4},{4,5},{5,6},{6,7},{8,9},{9,10},{10,11},{11... | collective-permute-start | bytes 61448 | tf_op jit(solution)/shard_map/ppermute | solution.py:22
  21.6 5.5 %collective-permute-start.2 = (bf16[40,32,2,4]{0,1,3,2:T(8,128)(2,1)S(1)}, bf16[40,32,2,4]{0,1,3,2:T(8,128)(2,1)S(1)}, u32[]{:S(2)}, u32[]{:S(2)}) collective-permute-start(bf16[40,32,2,4]{0,1,3,2:T(8,128)(2,1)S(1)} %copy.75), channel_id=1, source_target_pairs={{1,0},{2,1},{3,2},{4,3},{5,4},{6,5},{7,6},{9,8},{10,9},{11,10},{12... | collective-permute-start | bytes 61448 | tf_op jit(solution)/shard_map/ppermute | solution.py:22
  29.6 1.6 %copy-start = (bf16[5,8,64,384]{3,1,2,0:T(8,128)(2,1)}, bf16[5,8,64,384]{3,1,2,0:T(8,128)(2,1)S(1)}, u32[]{:S(2)}) copy-start(bf16[5,8,64,384]{3,1,2,0:T(8,128)(2,1)S(1)} %copy.116) | copy-start | bytes 5898244
  29.6 11.1 %copy-start.4 = (bf16[32,40,3,3,3]{1,0,4,3,2:T(8,128)(2,1)S(1)}, bf16[32,40,3,3,3]{1,0,4,3,2:T(8,128)(2,1)}, u32[]{:S(2)}) copy-start(bf16[32,40,3,3,3]{1,0,4,3,2:T(8,128)(2,1)} %param.14) | copy-start | bytes 207364
  31.3 11.7 %copy-start.7 = (f32[32]{0:T(128)S(1)}, f32[32]{0:T(128)}, u32[]{:S(2)}) copy-start(f32[32]{0:T(128)} %param.19) | copy-start | bytes 388
  31.3 11.7 %copy-start.8 = (f32[32]{0:T(128)S(1)}, f32[32]{0:T(128)}, u32[]{:S(2)}) copy-start(f32[32]{0:T(128)} %param.17) | copy-start | bytes 388
  31.3 11.7 %copy-start.9 = (f32[32]{0:T(128)S(1)}, f32[32]{0:T(128)}, u32[]{:S(2)}) copy-start(f32[32]{0:T(128)} %param.15) | copy-start | bytes 388
  31.3 28.6 %collective-permute-start.3 = (bf16[40,12288]{1,0:T(8,128)(2,1)}, bf16[40,12288]{1,0:T(8,128)(2,1)S(1)}, u32[]{:S(2)}, u32[]{:S(2)}) collective-permute-start(bf16[40,12288]{1,0:T(8,128)(2,1)} %get-tuple-element.6), channel_id=1, source_target_pairs={{0,8},{8,16},{16,24},{24,32},{32,40},{40,48},{48,56},{1,9},{9,17},... | collective-permute-start | bytes 2949128 | tf_op jit(solution)/shard_map/ppermute | solution.py:22
  34.9 26.5 %collective-permute-start.4 = (bf16[40,12288]{1,0:T(8,128)(2,1)S(1)}, bf16[40,12288]{1,0:T(8,128)(2,1)S(1)}, u32[]{:S(2)}, u32[]{:S(2)}) collective-permute-start(bf16[40,12288]{1,0:T(8,128)(2,1)S(1)} %get-tuple-element.5), channel_id=1, source_target_pairs={{8,0},{16,8},{24,16},{32,24},{40,32},{48,40},{56,48},{9,1},{17,9},... | collective-permute-start | bytes 2949128 | tf_op jit(solution)/shard_map/ppermute | solution.py:22
  59.9 1.5 copy-start.2
  61.4 1.0 copy-start.3
  68.4 9.9 %copy-start.5 = (bf16[32,32,3,3,3]{1,0,4,3,2:T(8,128)(2,1)S(1)}, bf16[32,32,3,3,3]{1,0,4,3,2:T(8,128)(2,1)}, u32[]{:S(2)}) copy-start(bf16[32,32,3,3,3]{1,0,4,3,2:T(8,128)(2,1)} %param.16) | copy-start | bytes 165892
  69.9 23.3 %collective-permute-start.5 = (bf16[32,11520]{1,0:T(8,128)(2,1)S(1)}, bf16[32,11520]{1,0:T(8,128)(2,1)S(1)}, u32[]{:S(2)}, u32[]{:S(2)}) collective-permute-start(bf16[32,11520]{1,0:T(8,128)(2,1)S(1)} %get-tuple-element.10), channel_id=1, source_target_pairs={{0,8},{8,16},{16,24},{24,32},{32,40},{40,48},{48,56},{1,9},{9,17},... | collective-permute-start | bytes 2211848 | tf_op jit(solution)/shard_map/ppermute | solution.py:22
  73.3 21.0 %collective-permute-start.6 = (bf16[32,11520]{1,0:T(8,128)(2,1)S(1)}, bf16[32,11520]{1,0:T(8,128)(2,1)S(1)}, u32[]{:S(2)}, u32[]{:S(2)}) collective-permute-start(bf16[32,11520]{1,0:T(8,128)(2,1)S(1)} %get-tuple-element.9), channel_id=1, source_target_pairs={{8,0},{16,8},{24,16},{32,24},{40,32},{48,40},{56,48},{9,1},{17,9},... | collective-permute-start | bytes 2211848 | tf_op jit(solution)/shard_map/ppermute | solution.py:22
  101.3 11.6 %copy-start.6 = (bf16[1,32,3,3,3]{1,4,3,2,0:T(4,128)(2,1)S(1)}, bf16[1,32,3,3,3]{1,4,3,2,0:T(4,128)(2,1)}, u32[]{:S(2)}) copy-start(bf16[1,32,3,3,3]{1,4,3,2,0:T(4,128)(2,1)} %param.20) | copy-start | bytes 5188
  102.7 21.3 %collective-permute-start.7 = (bf16[32,10752]{1,0:T(8,128)(2,1)S(1)}, bf16[32,10752]{1,0:T(8,128)(2,1)S(1)}, u32[]{:S(2)}, u32[]{:S(2)}) collective-permute-start(bf16[32,10752]{1,0:T(8,128)(2,1)S(1)} %get-tuple-element.8), channel_id=1, source_target_pairs={{0,8},{8,16},{16,24},{24,32},{32,40},{40,48},{48,56},{1,9},{9,17},... | collective-permute-start | bytes 2064392 | tf_op jit(solution)/shard_map/ppermute | solution.py:22
  105.0 20.2 %collective-permute-start.8 = (bf16[32,10752]{1,0:T(8,128)(2,1)S(1)}, bf16[32,10752]{1,0:T(8,128)(2,1)S(1)}, u32[]{:S(2)}, u32[]{:S(2)}) collective-permute-start(bf16[32,10752]{1,0:T(8,128)(2,1)S(1)} %get-tuple-element.7), channel_id=1, source_target_pairs={{8,0},{16,8},{24,16},{32,24},{40,32},{48,40},{56,48},{9,1},{17,9},... | collective-permute-start | bytes 2064392 | tf_op jit(solution)/shard_map/ppermute | solution.py:22
  142.1 8.4 %collective-permute-start.10 = (f32[24,256]{1,0:T(8,128)S(1)}, f32[24,256]{1,0:T(8,128)S(1)}, u32[]{:S(2)}, u32[]{:S(2)}) collective-permute-start(f32[24,256]{1,0:T(8,128)S(1)} %get-tuple-element.31), channel_id=1, source_target_pairs={{8,0},{16,8},{24,16},{32,24},{40,32},{48,40},{56,48},{9,1},{17,9},... | collective-permute-start | bytes 73736 | tf_op jit(solution)/shard_map/ppermute | solution.py:22
  148.6 7.8 %collective-permute-start.9 = (f32[24,256]{1,0:T(8,128)S(1)}, f32[24,256]{1,0:T(8,128)S(1)}, u32[]{:S(2)}, u32[]{:S(2)}) collective-permute-start(f32[24,256]{1,0:T(8,128)S(1)} %get-tuple-element.30), channel_id=1, source_target_pairs={{0,8},{8,16},{16,24},{24,32},{32,40},{40,48},{48,56},{1,9},{9,17},... | collective-permute-start | bytes 73736 | tf_op jit(solution)/shard_map/ppermute | solution.py:22

commit v3 on v2

--- a/solution.py
+++ b/solution.py
@@ -13,7 +13,7 @@
 PRE = 136
 LINE = 384
 DEPTH = 32
-STEP = 1536
+STEP = 768
 
 
 def from_behind(array, axis, by):
@@ -81,6 +81,8 @@
     limit = ref.shape[1]
     if start + size <= limit:
         return ref[:, start : start + size]
+    if start >= limit:
+        return jnp.zeros((ref.shape[0], size), ref.dtype)
     rest = jnp.zeros((ref.shape[0], start + size - limit), ref.dtype)
     return jnp.concatenate([ref[:, start:limit], rest], axis=1)
 

time: 158 us -> 158 us (level)
  no operation moved by 1% of the time
where the time goes in v3:
time: 158 us
  Pallas kernels  49 us (31%)
  starting transfers between devices  41.2 us (26%)
  waiting for transfers between devices  32.5 us (21%)
  local copies, waits for them, and re-layouts  25.8 us (16%)
  other arithmetic  7.33 us (5%)
  between operations  1.89 us (1%)
    ppermute x11, starting transfers between devices, from_behind(): return lax.ppermute(array, axis, pairs)  41.2 us
    ppermute x11, waiting for transfers between devices, from_behind(): return lax.ppermute(array, axis, pairs)  32.5 us
    pallas_call x3, Pallas kernels, conv_layer(): pl.pallas_call(functools.partial(halo_kernel, cout=rows_out, relu=relu, i...  19.8 us
    pallas_call x3, Pallas kernels, conv_layer(): pl.pallas_call(functools.partial(own_kernel, cout=rows_out), out_shape=ja...  16.3 us
    pallas_call x1, Pallas kernels, cost_head(): pl.pallas_call(functools.partial(own_kernel, cout=rows_out), out_shape=ja...  6.74 us
    pallas_call x1, Pallas kernels, correlate(): pl.pallas_call(correlate_kernel, out_shape=jax.ShapeDtypeStruct((rows, co...  6.2 us
    slice x3, local copies, waits for them, and re-layouts, conv_layer(): below = jnp.pad(from_behind(own[:sent, :span], 'row', -1), pad)  3.98 us
  transfers between devices with their start and end apart: 11, of which 9 were waited for; matrix products, arithmetic and copies ran while one was open for 10% of the time, Pallas kernels for 10%

profile of v3, /device:TPU:100, one launch (start us, length us, event | category | flops | bytes accessed | tf_op | source)
XLA Modules:
  0.0 157.7 jit_solution(12097937702986712367)
XLA Ops:
  0.0 1.0 copy.71
  1.0 0.2 slice.121
  1.2 1.9 %collective-permute-start = (bf16[320,2,136]{2,0,1:T(8,128)(2,1)S(1)}, bf16[320,2,136]{2,0,1:T(8,128)(2,1)S(1)}, u32[]{:S(2)}, u32[]{:S(2)}) collective-permute-start(bf16[320,2,136]{2,0,1:T(8,128)(2,1)S(1)} %slice.121), channel_id=1, source_target_pairs={{0,1},{1,2},{2,3},{3,4},{4,5},{5,6},{6,7},{8,9},{9,10},{10,11},{11... | collective-permute-start | bytes 522248 | tf_op jit(solution)/shard_map/ppermute | solution.py:22
  3.8 1.8 %copy.121 = bf16[40,8,2,256]{3,0,1,2:T(8,128)(2,1)} copy(bf16[40,8,2,256]{3,2,1,0:T(2,128)(2,1)} %bitcast.102) | data formatting | bytes 655360 | tf_op jit(solution)/shard_map/reshape | solution.py:71
  6.0 3.6 %collective-permute-done = bf16[320,2,136]{2,0,1:T(8,128)(2,1)S(1)} collective-permute-done((bf16[320,2,136]{2,0,1:T(8,128)(2,1)S(1)}, bf16[320,2,136]{2,0,1:T(8,128)(2,1)S(1)}, u32[]{:S(2)}, u32[]{:S(2)}) %collective-permute-start) | collective-permute-done | bytes 174112 | tf_op jit(solution)/shard_map/ppermute | solution.py:22
  9.6 0.4 fusion.2
  10.0 0.9 copy.120
  10.8 6.2 %shard_map.109 = bf16[2,32,40,256]{3,2,1,0:T(8,128)(2,1)} custom-call(bf16[2,8,40,256]{3,2,1,0:T(8,128)(2,1)} %bitcast.101, bf16[2,8,40,287]{3,2,1,0:T(8,128)(2,1)} %bitcast.100), custom_call_target="tpu_custom_call" | custom-call | tf_op jit(solution)/shard_map/pallas_call | solution.py:73
  17.0 1.5 fusion.29
  18.6 0.5 copy.74
  19.1 1.9 %collective-permute-start.1 = (bf16[40,32,2,4]{0,1,3,2:T(8,128)(2,1)S(1)}, bf16[40,32,2,4]{0,1,3,2:T(8,128)(2,1)S(1)}, u32[]{:S(2)}, u32[]{:S(2)}) collective-permute-start(bf16[40,32,2,4]{0,1,3,2:T(8,128)(2,1)S(1)} %copy.74), channel_id=1, source_target_pairs={{0,1},{1,2},{2,3},{3,4},{4,5},{5,6},{6,7},{8,9},{9,10},{10,11},{11... | collective-permute-start | bytes 61448 | tf_op jit(solution)/shard_map/ppermute | solution.py:22
  21.1 0.5 copy.75
  21.6 3.6 %collective-permute-start.2 = (bf16[40,32,2,4]{0,1,3,2:T(8,128)(2,1)S(1)}, bf16[40,32,2,4]{0,1,3,2:T(8,128)(2,1)S(1)}, u32[]{:S(2)}, u32[]{:S(2)}) collective-permute-start(bf16[40,32,2,4]{0,1,3,2:T(8,128)(2,1)S(1)} %copy.75), channel_id=1, source_target_pairs={{1,0},{2,1},{3,2},{4,3},{5,4},{6,5},{7,6},{9,8},{10,9},{11,10},{12... | collective-permute-start | bytes 61448 | tf_op jit(solution)/shard_map/ppermute | solution.py:22
  25.6 0.5 copy.76
  26.1 1.0 collective-permute-done.2
  27.2 0.5 copy.77
  27.7 1.3 maximum_bitcast_fusion
  28.9 0.5 pad_select_fusion
  29.4 0.2 copy.116
  29.7 1.1 fusion.26
  30.8 0.5 copy-done
  31.3 3.6 %collective-permute-start.3 = (bf16[40,12288]{1,0:T(8,128)(2,1)}, bf16[40,12288]{1,0:T(8,128)(2,1)S(1)}, u32[]{:S(2)}, u32[]{:S(2)}) collective-permute-start(bf16[40,12288]{1,0:T(8,128)(2,1)} %get-tuple-element.6), channel_id=1, source_target_pairs={{0,8},{8,16},{16,24},{24,32},{32,40},{40,48},{48,56},{1,9},{9,17},... | collective-permute-start | bytes 2949128 | tf_op jit(solution)/shard_map/ppermute | solution.py:22
  34.9 4.6 %collective-permute-start.4 = (bf16[40,12288]{1,0:T(8,128)(2,1)S(1)}, bf16[40,12288]{1,0:T(8,128)(2,1)S(1)}, u32[]{:S(2)}, u32[]{:S(2)}) collective-permute-start(bf16[40,12288]{1,0:T(8,128)(2,1)S(1)} %get-tuple-element.5), channel_id=1, source_target_pairs={{8,0},{16,8},{24,16},{32,24},{40,32},{48,40},{56,48},{9,1},{17,9},... | collective-permute-start | bytes 2949128 | tf_op jit(solution)/shard_map/ppermute | solution.py:22
  39.6 1.2 add_convert_fusion.keep_ref
  41.5 0.8 reshape.152.w_ref
  43.0 0.7 copy.84.b_ref
  43.7 0.7 pad_maximum_fusion.9.w_ref
  44.4 5.7 %shard_map.110.part_ref = f32[32,24576]{1,0:T(8,128)} custom-call(bf16[40,24576]{1,0:T(8,128)(2,1)} %bitcast.96, bf16[2,96,240]{2,1,0:T(8,128)(2,1)} %pad_maximum_fusion.9.w_ref), custom_call_target="tpu_custom_call" | custom-call | tf_op jit(solution)/shard_map/pallas_call | solution.py:160
  50.1 9.8 %collective-permute-done.3.above_ref = bf16[40,12288]{1,0:T(8,128)(2,1)S(1)} collective-permute-done((bf16[40,12288]{1,0:T(8,128)(2,1)}, bf16[40,12288]{1,0:T(8,128)(2,1)S(1)}, u32[]{:S(2)}, u32[]{:S(2)}) %collective-permute-start.3) | collective-permute-done | bytes 983072 | tf_op jit(solution)/shard_map/ppermute | solution.py:22
  59.9 1.5 collective-permute-done.4.below_ref
  61.4 1.0 copy-done.3
  62.4 6.2 %shard_map.111.x_ref.rest_0_ = bf16[32,24576]{1,0:T(8,128)(2,1)} custom-call(bf16[40,12288]{1,0:T(8,128)(2,1)} %copy-done.2, bf16[40,12288]{1,0:T(8,128)(2,1)} %copy-done.3, bf16[2,96,120]{2,1,0:T(8,128)(2,1)} %reshape.152.w_ref, f32[32,24576]{1,0:T(8,128)} %shard_map.110.part_ref, f32[4,32,1]{2,1,0:T(8,128)} %copy.84.b_ref, f32[4,24576]{1,0:T(4,128)} %add_convert_fusion.keep_ref), custom_call_target="tpu_custom_call" | custom-call | tf_op jit(solution)/shard_map/pallas_call | solution.py:171
  68.6 1.5 fusion.28
  70.1 3.4 %collective-permute-start.5 = (bf16[32,11520]{1,0:T(8,128)(2,1)S(1)}, bf16[32,11520]{1,0:T(8,128)(2,1)S(1)}, u32[]{:S(2)}, u32[]{:S(2)}) collective-permute-start(bf16[32,11520]{1,0:T(8,128)(2,1)S(1)} %get-tuple-element.10), channel_id=1, source_target_pairs={{0,8},{8,16},{16,24},{24,32},{32,40},{40,48},{48,56},{1,9},{9,17},... | collective-permute-start | bytes 2211848 | tf_op jit(solution)/shard_map/ppermute | solution.py:22
  73.5 5.0 %collective-permute-start.6 = (bf16[32,11520]{1,0:T(8,128)(2,1)S(1)}, bf16[32,11520]{1,0:T(8,128)(2,1)S(1)}, u32[]{:S(2)}, u32[]{:S(2)}) collective-permute-start(bf16[32,11520]{1,0:T(8,128)(2,1)S(1)} %get-tuple-element.9), channel_id=1, source_target_pairs={{8,0},{16,8},{24,16},{32,24},{40,32},{48,40},{56,48},{9,1},{17,9},... | collective-permute-start | bytes 2211848 | tf_op jit(solution)/shard_map/ppermute | solution.py:22
  79.0 0.1 stack.120
  79.3 0.8 reshape.153.w_ref
  80.1 0.6 pad_maximum_fusion.10.w_ref
  80.7 1.0 slice_bitcast_fusion.3
  81.8 5.3 %shard_map.112.part_ref = f32[32,24576]{1,0:T(8,128)} custom-call(bf16[32,24576]{1,0:T(8,128)(2,1)} %shard_map.111.x_ref.rest_0_, bf16[2,96,192]{2,1,0:T(8,128)(2,1)} %pad_maximum_fusion.10.w_ref), custom_call_target="tpu_custom_call" | custom-call | tf_op jit(solution)/shard_map/pallas_call | solution.py:160
  87.0 6.3 %collective-permute-done.5 = bf16[32,11520]{1,0:T(8,128)(2,1)S(1)} collective-permute-done((bf16[32,11520]{1,0:T(8,128)(2,1)S(1)}, bf16[32,11520]{1,0:T(8,128)(2,1)S(1)}, u32[]{:S(2)}, u32[]{:S(2)}) %collective-permute-start.5) | collective-permute-done | bytes 737312 | tf_op jit(solution)/shard_map/ppermute | solution.py:22
  93.4 0.9 pad.30.above_ref
  94.3 0.2 collective-permute-done.6
  94.5 0.9 pad.31.below_ref
  95.5 6.1 %shard_map.113.x_ref = bf16[32,24576]{1,0:T(8,128)(2,1)} custom-call(bf16[32,12288]{1,0:T(8,128)(2,1)} %pad.30.above_ref, bf16[32,12288]{1,0:T(8,128)(2,1)} %pad.31.below_ref, bf16[2,96,96]{2,1,0:T(8,128)(2,1)} %reshape.153.w_ref, f32[32,24576]{1,0:T(8,128)} %shard_map.112.part_ref, f32[4,32,1]{2,1,0:T(8,128)} %copy.84.b_ref, ...), custom_call_target="tpu_custom_call" | custom-call | tf_op jit(solution)/shard_map/pallas_call | solution.py:171
  101.6 1.4 fusion.27
  103.0 2.3 %collective-permute-start.7 = (bf16[32,10752]{1,0:T(8,128)(2,1)S(1)}, bf16[32,10752]{1,0:T(8,128)(2,1)S(1)}, u32[]{:S(2)}, u32[]{:S(2)}) collective-permute-start(bf16[32,10752]{1,0:T(8,128)(2,1)S(1)} %get-tuple-element.8), channel_id=1, source_target_pairs={{0,8},{8,16},{16,24},{24,32},{32,40},{40,48},{48,56},{1,9},{9,17},... | collective-permute-start | bytes 2064392 | tf_op jit(solution)/shard_map/ppermute | solution.py:22
  105.3 6.4 %collective-permute-start.8 = (bf16[32,10752]{1,0:T(8,128)(2,1)S(1)}, bf16[32,10752]{1,0:T(8,128)(2,1)S(1)}, u32[]{:S(2)}, u32[]{:S(2)}) collective-permute-start(bf16[32,10752]{1,0:T(8,128)(2,1)S(1)} %get-tuple-element.7), channel_id=1, source_target_pairs={{8,0},{16,8},{24,16},{32,24},{40,32},{48,40},{56,48},{9,1},{17,9},... | collective-permute-start | bytes 2064392 | tf_op jit(solution)/shard_map/ppermute | solution.py:22
  111.9 0.1 stack.124
  112.5 0.8 reshape.154.w_ref
  114.0 0.6 pad_maximum_fusion.14.w_ref
  114.6 0.7 pad_maximum_fusion.11.w_ref
  115.3 5.3 %shard_map.114.part_ref = f32[32,24576]{1,0:T(8,128)} custom-call(bf16[32,24576]{1,0:T(8,128)(2,1)} %shard_map.113.x_ref, bf16[2,96,192]{2,1,0:T(8,128)(2,1)} %pad_maximum_fusion.11.w_ref), custom_call_target="tpu_custom_call" | custom-call | tf_op jit(solution)/shard_map/pallas_call | solution.py:160
  120.5 3.9 %collective-permute-done.7 = bf16[32,10752]{1,0:T(8,128)(2,1)S(1)} collective-permute-done((bf16[32,10752]{1,0:T(8,128)(2,1)S(1)}, bf16[32,10752]{1,0:T(8,128)(2,1)S(1)}, u32[]{:S(2)}, u32[]{:S(2)}) %collective-permute-start.7) | collective-permute-done | bytes 688160 | tf_op jit(solution)/shard_map/ppermute | solution.py:22
  124.4 0.9 pad.32.above_ref
  125.3 0.2 collective-permute-done.8
  125.6 0.9 pad.33.below_ref
  126.5 7.4 %shard_map.115.x_ref = bf16[32,24576]{1,0:T(8,128)(2,1)} custom-call(bf16[32,12288]{1,0:T(8,128)(2,1)} %pad.32.above_ref, bf16[32,12288]{1,0:T(8,128)(2,1)} %pad.33.below_ref, bf16[2,96,96]{2,1,0:T(8,128)(2,1)} %reshape.154.w_ref, f32[32,24576]{1,0:T(8,128)} %shard_map.114.part_ref, f32[4,32,1]{2,1,0:T(8,128)} %copy.84.b_ref, ...), custom_call_target="tpu_custom_call" | custom-call | tf_op jit(solution)/shard_map/pallas_call | solution.py:171
  133.9 6.7 %shard_map.116 = f32[8,49152]{1,0:T(8,128)} custom-call(bf16[32,24576]{1,0:T(8,128)(2,1)} %shard_map.115.x_ref, bf16[4,24,192]{2,1,0:T(8,128)(2,1)} %pad_maximum_fusion.14.w_ref), custom_call_target="tpu_custom_call" | custom-call | tf_op jit(solution)/shard_map/pallas_call | solution.py:259
  140.6 1.9 %slice_reduce_fusion = f32[49152]{0:T(1024)S(1)} fusion(f32[8,49152]{1,0:T(8,128)} %shard_map.116), kind=kLoop, calls=%fused_computation.10 | loop fusion | bytes 393216 | tf_op jit(solution)/shard_map/slice | solution.py:263
  142.6 6.5 %collective-permute-start.10 = (f32[24,256]{1,0:T(8,128)S(1)}, f32[24,256]{1,0:T(8,128)S(1)}, u32[]{:S(2)}, u32[]{:S(2)}) collective-permute-start(f32[24,256]{1,0:T(8,128)S(1)} %get-tuple-element.31), channel_id=1, source_target_pairs={{8,0},{16,8},{24,16},{32,24},{40,32},{48,40},{56,48},{9,1},{17,9},... | collective-permute-start | bytes 73736 | tf_op jit(solution)/shard_map/ppermute | solution.py:22
  149.1 1.9 %collective-permute-start.9 = (f32[24,256]{1,0:T(8,128)S(1)}, f32[24,256]{1,0:T(8,128)S(1)}, u32[]{:S(2)}, u32[]{:S(2)}) collective-permute-start(f32[24,256]{1,0:T(8,128)S(1)} %get-tuple-element.30), channel_id=1, source_target_pairs={{0,8},{8,16},{16,24},{24,32},{32,40},{40,48},{48,56},{1,9},{9,17},... | collective-permute-start | bytes 73736 | tf_op jit(solution)/shard_map/ppermute | solution.py:22
  151.0 5.9 %collective-permute-done.9 = f32[24,256]{1,0:T(8,128)S(1)} collective-permute-done((f32[24,256]{1,0:T(8,128)S(1)}, f32[24,256]{1,0:T(8,128)S(1)}, u32[]{:S(2)}, u32[]{:S(2)}) %collective-permute-start.9) | collective-permute-done | bytes 24608 | tf_op jit(solution)/shard_map/ppermute | solution.py:22
  157.0 0.7 fusion.3
  (80 shorter events, 3.5 us)
Async XLA Ops:
  1.2 8.4 %collective-permute-start = (bf16[320,2,136]{2,0,1:T(8,128)(2,1)S(1)}, bf16[320,2,136]{2,0,1:T(8,128)(2,1)S(1)}, u32[]{:S(2)}, u32[]{:S(2)}) collective-permute-start(bf16[320,2,136]{2,0,1:T(8,128)(2,1)S(1)} %slice.121), channel_id=1, source_target_pairs={{0,1},{1,2},{2,3},{3,4},{4,5},{5,6},{6,7},{8,9},{9,10},{10,11},{11... | collective-permute-start | bytes 522248 | tf_op jit(solution)/shard_map/ppermute | solution.py:22
  18.6 9.1 %copy-start.1 = (bf16[2,32,40,256]{3,2,1,0:T(8,128)(2,1)S(1)}, bf16[2,32,40,256]{3,2,1,0:T(8,128)(2,1)}, u32[]{:S(2)}) copy-start(bf16[2,32,40,256]{3,2,1,0:T(8,128)(2,1)} %shard_map.109) | copy-start | bytes 3932164
  19.1 6.5 %collective-permute-start.1 = (bf16[40,32,2,4]{0,1,3,2:T(8,128)(2,1)S(1)}, bf16[40,32,2,4]{0,1,3,2:T(8,128)(2,1)S(1)}, u32[]{:S(2)}, u32[]{:S(2)}) collective-permute-start(bf16[40,32,2,4]{0,1,3,2:T(8,128)(2,1)S(1)} %copy.74), channel_id=1, source_target_pairs={{0,1},{1,2},{2,3},{3,4},{4,5},{5,6},{6,7},{8,9},{9,10},{10,11},{11... | collective-permute-start | bytes 61448 | tf_op jit(solution)/shard_map/ppermute | solution.py:22
  21.6 5.5 %collective-permute-start.2 = (bf16[40,32,2,4]{0,1,3,2:T(8,128)(2,1)S(1)}, bf16[40,32,2,4]{0,1,3,2:T(8,128)(2,1)S(1)}, u32[]{:S(2)}, u32[]{:S(2)}) collective-permute-start(bf16[40,32,2,4]{0,1,3,2:T(8,128)(2,1)S(1)} %copy.75), channel_id=1, source_target_pairs={{1,0},{2,1},{3,2},{4,3},{5,4},{6,5},{7,6},{9,8},{10,9},{11,10},{12... | collective-permute-start | bytes 61448 | tf_op jit(solution)/shard_map/ppermute | solution.py:22
  29.6 1.6 %copy-start = (bf16[5,8,64,384]{3,1,2,0:T(8,128)(2,1)}, bf16[5,8,64,384]{3,1,2,0:T(8,128)(2,1)S(1)}, u32[]{:S(2)}) copy-start(bf16[5,8,64,384]{3,1,2,0:T(8,128)(2,1)S(1)} %copy.116) | copy-start | bytes 5898244
  29.6 11.1 %copy-start.4 = (bf16[32,40,3,3,3]{1,0,4,3,2:T(8,128)(2,1)S(1)}, bf16[32,40,3,3,3]{1,0,4,3,2:T(8,128)(2,1)}, u32[]{:S(2)}) copy-start(bf16[32,40,3,3,3]{1,0,4,3,2:T(8,128)(2,1)} %param.14) | copy-start | bytes 207364
  31.3 11.7 %copy-start.7 = (f32[32]{0:T(128)S(1)}, f32[32]{0:T(128)}, u32[]{:S(2)}) copy-start(f32[32]{0:T(128)} %param.19) | copy-start | bytes 388
  31.3 11.7 %copy-start.8 = (f32[32]{0:T(128)S(1)}, f32[32]{0:T(128)}, u32[]{:S(2)}) copy-start(f32[32]{0:T(128)} %param.17) | copy-start | bytes 388
  31.3 11.7 %copy-start.9 = (f32[32]{0:T(128)S(1)}, f32[32]{0:T(128)}, u32[]{:S(2)}) copy-start(f32[32]{0:T(128)} %param.15) | copy-start | bytes 388
  31.3 28.6 %collective-permute-start.3 = (bf16[40,12288]{1,0:T(8,128)(2,1)}, bf16[40,12288]{1,0:T(8,128)(2,1)S(1)}, u32[]{:S(2)}, u32[]{:S(2)}) collective-permute-start(bf16[40,12288]{1,0:T(8,128)(2,1)} %get-tuple-element.6), channel_id=1, source_target_pairs={{0,8},{8,16},{16,24},{24,32},{32,40},{40,48},{48,56},{1,9},{9,17},... | collective-permute-start | bytes 2949128 | tf_op jit(solution)/shard_map/ppermute | solution.py:22
  34.9 26.5 %collective-permute-start.4 = (bf16[40,12288]{1,0:T(8,128)(2,1)S(1)}, bf16[40,12288]{1,0:T(8,128)(2,1)S(1)}, u32[]{:S(2)}, u32[]{:S(2)}) collective-permute-start(bf16[40,12288]{1,0:T(8,128)(2,1)S(1)} %get-tuple-element.5), channel_id=1, source_target_pairs={{8,0},{16,8},{24,16},{32,24},{40,32},{48,40},{56,48},{9,1},{17,9},... | collective-permute-start | bytes 2949128 | tf_op jit(solution)/shard_map/ppermute | solution.py:22
  59.9 1.5 copy-start.2
  61.4 1.0 copy-start.3
  68.6 9.9 %copy-start.5 = (bf16[32,32,3,3,3]{1,0,4,3,2:T(8,128)(2,1)S(1)}, bf16[32,32,3,3,3]{1,0,4,3,2:T(8,128)(2,1)}, u32[]{:S(2)}) copy-start(bf16[32,32,3,3,3]{1,0,4,3,2:T(8,128)(2,1)} %param.16) | copy-start | bytes 165892
  70.1 23.3 %collective-permute-start.5 = (bf16[32,11520]{1,0:T(8,128)(2,1)S(1)}, bf16[32,11520]{1,0:T(8,128)(2,1)S(1)}, u32[]{:S(2)}, u32[]{:S(2)}) collective-permute-start(bf16[32,11520]{1,0:T(8,128)(2,1)S(1)} %get-tuple-element.10), channel_id=1, source_target_pairs={{0,8},{8,16},{16,24},{24,32},{32,40},{40,48},{48,56},{1,9},{9,17},... | collective-permute-start | bytes 2211848 | tf_op jit(solution)/shard_map/ppermute | solution.py:22
  73.5 21.0 %collective-permute-start.6 = (bf16[32,11520]{1,0:T(8,128)(2,1)S(1)}, bf16[32,11520]{1,0:T(8,128)(2,1)S(1)}, u32[]{:S(2)}, u32[]{:S(2)}) collective-permute-start(bf16[32,11520]{1,0:T(8,128)(2,1)S(1)} %get-tuple-element.9), channel_id=1, source_target_pairs={{8,0},{16,8},{24,16},{32,24},{40,32},{48,40},{56,48},{9,1},{17,9},... | collective-permute-start | bytes 2211848 | tf_op jit(solution)/shard_map/ppermute | solution.py:22
  101.6 11.6 %copy-start.6 = (bf16[1,32,3,3,3]{1,4,3,2,0:T(4,128)(2,1)S(1)}, bf16[1,32,3,3,3]{1,4,3,2,0:T(4,128)(2,1)}, u32[]{:S(2)}) copy-start(bf16[1,32,3,3,3]{1,4,3,2,0:T(4,128)(2,1)} %param.20) | copy-start | bytes 5188
  103.0 21.4 %collective-permute-start.7 = (bf16[32,10752]{1,0:T(8,128)(2,1)S(1)}, bf16[32,10752]{1,0:T(8,128)(2,1)S(1)}, u32[]{:S(2)}, u32[]{:S(2)}) collective-permute-start(bf16[32,10752]{1,0:T(8,128)(2,1)S(1)} %get-tuple-element.8), channel_id=1, source_target_pairs={{0,8},{8,16},{16,24},{24,32},{32,40},{40,48},{48,56},{1,9},{9,17},... | collective-permute-start | bytes 2064392 | tf_op jit(solution)/shard_map/ppermute | solution.py:22
  105.3 20.2 %collective-permute-start.8 = (bf16[32,10752]{1,0:T(8,128)(2,1)S(1)}, bf16[32,10752]{1,0:T(8,128)(2,1)S(1)}, u32[]{:S(2)}, u32[]{:S(2)}) collective-permute-start(bf16[32,10752]{1,0:T(8,128)(2,1)S(1)} %get-tuple-element.7), channel_id=1, source_target_pairs={{8,0},{16,8},{24,16},{32,24},{40,32},{48,40},{56,48},{9,1},{17,9},... | collective-permute-start | bytes 2064392 | tf_op jit(solution)/shard_map/ppermute | solution.py:22
  142.6 8.5 %collective-permute-start.10 = (f32[24,256]{1,0:T(8,128)S(1)}, f32[24,256]{1,0:T(8,128)S(1)}, u32[]{:S(2)}, u32[]{:S(2)}) collective-permute-start(f32[24,256]{1,0:T(8,128)S(1)} %get-tuple-element.31), channel_id=1, source_target_pairs={{8,0},{16,8},{24,16},{32,24},{40,32},{48,40},{56,48},{9,1},{17,9},... | collective-permute-start | bytes 73736 | tf_op jit(solution)/shard_map/ppermute | solution.py:22
  149.1 7.8 %collective-permute-start.9 = (f32[24,256]{1,0:T(8,128)S(1)}, f32[24,256]{1,0:T(8,128)S(1)}, u32[]{:S(2)}, u32[]{:S(2)}) collective-permute-start(f32[24,256]{1,0:T(8,128)S(1)} %get-tuple-element.30), channel_id=1, source_target_pairs={{0,8},{8,16},{16,24},{24,32},{32,40},{40,48},{48,56},{1,9},{9,17},... | collective-permute-start | bytes 73736 | tf_op jit(solution)/shard_map/ppermute | solution.py:22
